TPU v7x, 32 devices: a whole 2x2x4 slice. The times are simulated.
32 devices in a mesh: node: 4 (over y, core), local: 8 (over z, x).
Axes of the slice: x: 2, y: 2, z: 4, core: 2. Of those that a mesh axis runs over, the one named last changes fastest.
Arguments:
- tokens: bfloat16 [4096, 4096], P(('node', 'local')), may hold values from -6 to 6
- grad_out: bfloat16 [4096, 4096], P(('node', 'local')), may hold values from -6 to 6
- expert_ids: int32 [4096, 4], P(('node', 'local')), may hold values from 0 to 31, all different within a row; in each aligned block of 128 rows (0 to 127, 128 to 255, ...) at most 20 rows name the same one
- combine_w: float32 [4096, 4], P(('node', 'local')), may hold values from 0.1 to 0.6
- w_gate: bfloat16 [32, 4096, 768], P(('node', 'local')), may hold values from -0.09375 to 0.09375
- w_up: bfloat16 [32, 4096, 768], P(('node', 'local')), may hold values from -0.09375 to 0.09375
- w_down: bfloat16 [32, 768, 4096], P(('node', 'local')), may hold values from -0.21875 to 0.21875
Outputs:
- mixed: bfloat16 [4096, 4096], P(('node', 'local'))
- grad_in: bfloat16 [4096, 4096], P(('node', 'local'))
Inputs may be any that keep to these rules, and one draw needn't show every extreme that they name: `expert_ids`: each row names 4 different experts. Among the 128 rows of one device no expert is named more than 20 times, and in every draw some device names some expert exactly 20 times.
All inputs are finite; a program needn't handle non-finite values.
Results may differ from a plain program's by a relative error of at most 0.0058.
Values may be sent and summed in bfloat16 or wider, within the bound.
No kernel may reach another device: no remote copies, remote signals or barrier semaphores. Data moves between devices by JAX's collectives and lax.ppermute only.
A program may use at most 128 MiB of HBM per device.

v0:
```python
import jax
import jax.numpy as jnp
from jax import lax
from jax.sharding import PartitionSpec as P


def expert_rows(rows, gate_w, up_w, down_w, width):
    inputs = rows[:, :width]
    upstream = rows[:, width:]
    gate = jnp.dot(inputs, gate_w, preferred_element_type=jnp.float32)
    lifted = jnp.dot(inputs, up_w, preferred_element_type=jnp.float32)
    sigma = jax.nn.sigmoid(gate)
    active = (gate * sigma * lifted).astype(jnp.bfloat16)
    result = jnp.dot(active, down_w, preferred_element_type=jnp.float32).astype(jnp.bfloat16)
    contract = (((1,), (1,)), ((), ()))
    back = lax.dot_general(upstream, down_w, contract, preferred_element_type=jnp.float32)
    d_gate = (back * lifted * sigma * (1.0 + gate * (1.0 - sigma))).astype(jnp.bfloat16)
    d_lift = (back * gate * sigma).astype(jnp.bfloat16)
    grads = lax.dot_general(d_gate, gate_w, contract, preferred_element_type=jnp.float32)
    grads = grads + lax.dot_general(d_lift, up_w, contract, preferred_element_type=jnp.float32)
    return jnp.concatenate([result, grads.astype(jnp.bfloat16)], axis=1)


def row_slots(expert_ids, experts, capacity):
    flat_ids = expert_ids.reshape(-1)
    onehot = (flat_ids[:, None] == jnp.arange(experts, dtype=jnp.int32)[None, :]).astype(jnp.int32)
    ranks = jnp.sum((jnp.cumsum(onehot, axis=0) - 1) * onehot, axis=1)
    return flat_ids * capacity + ranks


def outward(buffer):
    return lax.all_to_all(buffer, ("node", "local"), split_axis=0, concat_axis=0, tiled=True)


def homeward(buffer):
    return lax.all_to_all(buffer, ("node", "local"), split_axis=0, concat_axis=0, tiled=True)


def per_device(tokens, grad_out, expert_ids, combine_w, w_gate, w_up, w_down):
    token_count, width = tokens.shape
    top_count = expert_ids.shape[1]
    experts = lax.axis_size("node") * lax.axis_size("local")
    capacity = max(2, (5 * token_count * top_count + 4 * experts - 1) // (4 * experts))
    slots = row_slots(expert_ids, experts, capacity)
    owners = jnp.arange(token_count * top_count, dtype=jnp.int32) // top_count
    paired = jnp.concatenate([tokens, grad_out], axis=1)
    buffer = jnp.zeros((experts * capacity, 2 * width), jnp.bfloat16).at[slots].set(paired[owners])
    received = outward(buffer.reshape(experts, capacity, 2 * width))
    received = received.reshape(experts * capacity, 2 * width)
    produced = expert_rows(received, w_gate[0], w_up[0], w_down[0], width)
    returned = homeward(produced.reshape(experts, capacity, 2 * width))
    returned = returned.reshape(experts * capacity, 2 * width)
    picked = returned[slots].astype(jnp.float32) * combine_w.reshape(-1)[:, None]
    summed = jnp.sum(picked.reshape(token_count, top_count, 2 * width), axis=1)
    return (summed[:, :width].astype(jnp.bfloat16), summed[:, width:].astype(jnp.bfloat16))


def solution(mesh):
    return jax.shard_map(
        per_device,
        mesh=mesh,
        in_specs=(
            P(("node", "local"), None),
            P(("node", "local"), None),
            P(("node", "local"), None),
            P(("node", "local"), None),
            P(("node", "local"), None, None),
            P(("node", "local"), None, None),
            P(("node", "local"), None, None),
        ),
        out_specs=(P(("node", "local"), None), P(("node", "local"), None)),
        check_vma=False,
    )
```

profile of v0, /device:TPU:0, one launch (start us, length us, event | category | flops | bytes accessed | tf_op | source)
XLA Modules:
  0.0 769.2 jit_solution(17316934694007833266)
XLA Ops:
  0.6 0.8 copy.11
  2.3 1.2 reduce-window.6
  4.1 1.7 pad_maximum_fusion.1
  5.8 7.8 %gather_fusion = bf16[512,8192]{1,0:T(8,128)(2,1)} fusion(bf16[128,8192]{1,0:T(8,128)(2,1)S(1)} %pad_maximum_fusion.1, s32[1024]{0:T(1024)S(1)} %pad_clamp_fusion.1), kind=kCustom, calls=%fused_computation | custom fusion | bytes 16779264 | tf_op jit(solution)/shard_map/gather | solution.py:47
  13.6 20.0 %scatter_custom_fusion = bf16[640,8192]{1,0:T(8,128)(2,1)} fusion(s32[512]{0:T(512)S(1)} %bitcast.33, bf16[512,8192]{1,0:T(8,128)(2,1)} %gather_fusion, bf16[]{:T(256)} %constant.27.clone.1), kind=kCustom, calls=%fused_computation.18 | custom fusion | bytes 10486272 | tf_op jit(solution)/shard_map/scatter | solution.py:47
  33.7 14.1 %reshape.118 = bf16[32,20,8192]{2,1,0:T(8,128)(2,1)} reshape(bf16[640,8192]{1,0:T(8,128)(2,1)} %scatter_custom_fusion) | data formatting | bytes 20971520 | tf_op jit(solution)/shard_map/reshape | solution.py:48
  47.8 282.2 %all_to_all.10 = bf16[32,20,8192]{2,1,0:T(8,128)(2,1)} all-to-all(bf16[32,20,8192]{2,1,0:T(8,128)(2,1)} %reshape.118), channel_id=1, replica_groups=mesh['node'=4,'local'=8] {'node','local'}, dimensions={0} | all-to-all | bytes 20971520 | tf_op jit(solution)/shard_map/all_to_all | solution.py:32
  329.9 14.4 %reshape.119 = bf16[640,8192]{1,0:T(8,128)(2,1)} reshape(bf16[32,20,8192]{2,1,0:T(8,128)(2,1)} %all_to_all.10) | data formatting | bytes 20971520 | tf_op jit(solution)/shard_map/reshape | solution.py:49
  344.4 10.0 %fusion.8 = f32[640,768]{1,0:T(8,128)} fusion(bf16[1,4096,768]{2,1,0:T(8,128)(2,1)} %param.11, bf16[640,8192]{1,0:T(8,128)(2,1)} %reshape.119), kind=kOutput, calls=%fused_computation.15 | convolution fusion | flops 4026531840 | bytes 13500416 | tf_op jit(solution)/shard_map/dot_general | solution.py:10
  354.4 5.5 fusion
  359.9 6.5 fusion.4
  366.5 1.3 copy-done.4
  367.8 5.0 convolution_convert_fusion
  372.8 12.2 %fusion.6 = f32[640,4096]{1,0:T(8,128)} fusion(bf16[1,4096,768]{2,1,0:T(8,128)(2,1)} %param.11, f32[640,768]{1,0:T(8,128)S(1)} %copy-done.2, f32[640,768]{1,0:T(8,128)S(1)} %copy-done.3, f32[640,768]{1,0:T(8,128)} %copy-done.4), kind=kOutput, calls=%fused_computation.13 | convolution fusion | flops 4031447040 | bytes 22675456 | tf_op jit(solution)/shard_map/dot_general | solution.py:19
  384.9 13.5 %add_convert_fusion = bf16[640,4096]{1,0:T(8,128)(2,1)} fusion(f32[640,4096]{1,0:T(8,128)} %fusion.6, bf16[1,4096,768]{2,1,0:T(8,128)(2,1)} %param.12, f32[640,768]{1,0:T(8,128)} %fusion, f32[640,768]{1,0:T(8,128)} %fusion.8), kind=kOutput, calls=%fused_computation.5 | convolution fusion | flops 4034723840 | bytes 25952256 | tf_op jit(solution)/shard_map/dot_general | solution.py:20
  398.5 7.2 pad_maximum_fusion
  405.7 14.0 %reshape.120 = bf16[32,20,8192]{2,1,0:T(8,128)(2,1)} reshape(bf16[640,8192]{1,0:T(8,128)(2,1)} %pad_maximum_fusion) | data formatting | bytes 20971520 | tf_op jit(solution)/shard_map/reshape | solution.py:51
  419.7 4.1 all-to-all-start.1
  423.9 279.3 %all-to-all-done.1 = bf16[32,20,8192]{2,1,0:T(8,128)(2,1)} async-done(((bf16[32,20,8192]{2,1,0:T(8,128)(2,1)}), bf16[32,20,8192]{2,1,0:T(8,128)(2,1)}, u32[]{:S(2)}, u32[]{:S(2)}) %all-to-all-start.1) | async-done | bytes 10485792 | tf_op jit(solution)/shard_map/all_to_all | solution.py:36
  703.1 14.2 %reshape.121 = bf16[640,8192]{1,0:T(8,128)(2,1)} reshape(bf16[32,20,8192]{2,1,0:T(8,128)(2,1)} %all-to-all-done.1) | data formatting | bytes 20971520 | tf_op jit(solution)/shard_map/reshape | solution.py:52
  717.3 20.8 %gather_fusion.1 = bf16[512,8192]{1,0:T(8,128)(2,1)} fusion(bf16[640,8192]{1,0:T(8,128)(2,1)} %reshape.121, s32[1024]{0:T(1024)S(1)} %pad_clamp_fusion), kind=kCustom, calls=%fused_computation.1 | custom fusion | bytes 16779264 | tf_op jit(solution)/shard_map/gather | solution.py:53
  738.1 15.5 %reshape.122 = f32[128,4,8192]{2,1,0:T(4,128)} reshape(bf16[512,8192]{1,0:T(8,128)(2,1)} %gather_fusion.1) | data formatting | bytes 25165824 | tf_op jit(solution)/shard_map/convert_element_type | solution.py:53
  753.6 13.9 %multiply_reduce_fusion = bf16[128,8192]{1,0:T(8,128)(2,1)S(1)} fusion(f32[128,4,8192]{2,1,0:T(4,128)} %reshape.122, f32[128,4]{1,0:T(8,128)S(1)} %copy.14), kind=kLoop, calls=%fused_computation.3 | loop fusion | flops 7340032 | bytes 18876416 | tf_op jit(solution)/shard_map/reduce_sum | solution.py:54
  767.6 1.5 fusion.24
  (34 shorter events, 1.7 us)
Async XLA Ops:
  329.9 24.4 %slice-start = ((s8[6291456]{0:T(1024)(128)(4,1)}), s8[2097152]{0:T(1024)(128)(4,1)S(1)}, s32[]{:S(2)}) async-start(s8[6291456]{0:T(1024)(128)(4,1)} %bitcast.37), calls=%async_computation.2 | async-start | bytes 4194304
  344.4 10.0 %copy-start = (bf16[640,8192]{1,0:T(8,128)(2,1)S(1)}, bf16[640,8192]{1,0:T(8,128)(2,1)}, u32[]{:S(2)}) copy-start(bf16[640,8192]{1,0:T(8,128)(2,1)} %reshape.119) | copy-start | bytes 31457284
  344.4 10.0 %slice-start.1 = ((s8[6291456]{0:T(1024)(128)(4,1)}), s8[4194304]{0:T(1024)(128)(4,1)S(1)}, s32[]{:S(2)}) async-start(s8[6291456]{0:T(1024)(128)(4,1)} %bitcast.37), calls=%async_computation.3 | async-start | bytes 8388608
  354.4 13.4 %slice-start.2 = ((s8[6291456]{0:T(1024)(128)(4,1)}), s8[4194304]{0:T(1024)(128)(4,1)S(1)}, s32[]{:S(2)}) async-start(s8[6291456]{0:T(1024)(128)(4,1)} %bitcast.39), calls=%async_computation.4 | async-start | bytes 8388608
  359.9 7.8 %slice-start.3 = ((s8[6291456]{0:T(1024)(128)(4,1)}), s8[2097152]{0:T(1024)(128)(4,1)S(1)}, s32[]{:S(2)}) async-start(s8[6291456]{0:T(1024)(128)(4,1)} %bitcast.39), calls=%async_computation.5 | async-start | bytes 4194304
  359.9 7.8 %copy-start.2 = (f32[640,768]{1,0:T(8,128)S(1)}, f32[640,768]{1,0:T(8,128)}, u32[]{:S(2)}) copy-start(f32[640,768]{1,0:T(8,128)} %fusion.8) | copy-start | bytes 5898244
  366.5 1.3 copy-start.4
  367.8 5.0 copy-start.3
  419.7 4.1 copy-start.1
  419.7 283.5 %all-to-all-start.1 = ((bf16[32,20,8192]{2,1,0:T(8,128)(2,1)}), bf16[32,20,8192]{2,1,0:T(8,128)(2,1)}, u32[]{:S(2)}, u32[]{:S(2)}) async-start(bf16[32,20,8192]{2,1,0:T(8,128)(2,1)} %reshape.120), calls=%async_computation.1 | async-start | bytes 25165824 | tf_op jit(solution)/shard_map/all_to_all | solution.py:36
where the time goes:
time: 780 us; the launch traced here: 769 us
  blocking collectives  282 us (36%)
  waiting for transfers between devices  279 us (36%)
  local copies, waits for them, and re-layouts  125 us (16%)
  matrix products  52.7 us (7%)
  other arithmetic  24.9 us (3%)
    all_to_all x1, blocking collectives, outward(): lax.all_to_all(buffer, ('node', 'local'), split_axis=0, concat_axis=0, ti...  282 us
    all_to_all x1, waiting for transfers between devices, homeward(): lax.all_to_all(buffer, ('node', 'local'), split_axis=0, concat_axis=0, ti...  279 us
    gather x1, local copies, waits for them, and re-layouts, per_device(): returned[slots].astype(jnp.float32) * combine_w.reshape(-1)[:, None]  20.8 us
    scatter x1, local copies, waits for them, and re-layouts, per_device(): jnp.zeros((experts * capacity, 2 * width), jnp.bfloat16).at[slots]  20 us
  transfers between devices with their start and end apart: 1, of which 1 were waited for; matrix products, arithmetic and copies ran while one was open for 0% of the time, Pallas kernels for 0%

commit v1 on v0

--- a/solution.py
+++ b/solution.py
@@ -36,22 +36,36 @@
     return lax.all_to_all(buffer, ("node", "local"), split_axis=0, concat_axis=0, tiled=True)
 
 
+def split_three(weights):
+    high = weights.astype(jnp.bfloat16)
+    rest = weights - high.astype(jnp.float32)
+    middle = rest.astype(jnp.bfloat16)
+    low = (rest - middle.astype(jnp.float32)).astype(jnp.bfloat16)
+    return high, middle, low
+
+
 def per_device(tokens, grad_out, expert_ids, combine_w, w_gate, w_up, w_down):
     token_count, width = tokens.shape
     top_count = expert_ids.shape[1]
     experts = lax.axis_size("node") * lax.axis_size("local")
     capacity = max(2, (5 * token_count * top_count + 4 * experts - 1) // (4 * experts))
-    slots = row_slots(expert_ids, experts, capacity)
-    owners = jnp.arange(token_count * top_count, dtype=jnp.int32) // top_count
+    slots_per = (capacity + 7) // 8 * 8
+    total_slots = experts * slots_per
+    slots = row_slots(expert_ids, experts, slots_per).reshape(token_count, top_count)
+    hits = slots[None, :, :] == jnp.arange(total_slots, dtype=jnp.int32)[:, None, None]
+    dispatch = jnp.any(hits, axis=2).astype(jnp.bfloat16)
     paired = jnp.concatenate([tokens, grad_out], axis=1)
-    buffer = jnp.zeros((experts * capacity, 2 * width), jnp.bfloat16).at[slots].set(paired[owners])
-    received = outward(buffer.reshape(experts, capacity, 2 * width))
-    received = received.reshape(experts * capacity, 2 * width)
+    buffer = jnp.dot(dispatch, paired, preferred_element_type=jnp.float32).astype(jnp.bfloat16)
+    received = outward(buffer.reshape(experts, slots_per, 2 * width))
+    received = received.reshape(total_slots, 2 * width)
     produced = expert_rows(received, w_gate[0], w_up[0], w_down[0], width)
-    returned = homeward(produced.reshape(experts, capacity, 2 * width))
-    returned = returned.reshape(experts * capacity, 2 * width)
-    picked = returned[slots].astype(jnp.float32) * combine_w.reshape(-1)[:, None]
-    summed = jnp.sum(picked.reshape(token_count, top_count, 2 * width), axis=1)
+    returned = homeward(produced.reshape(experts, slots_per, 2 * width))
+    returned = returned.reshape(total_slots, 2 * width)
+    spread = jnp.where(hits, combine_w[None, :, :], 0.0).sum(axis=2).T
+    summed = None
+    for part in split_three(spread):
+        term = jnp.dot(part, returned, preferred_element_type=jnp.float32)
+        summed = term if summed is None else summed + term
     return (summed[:, :width].astype(jnp.bfloat16), summed[:, width:].astype(jnp.bfloat16))
 
 

time: 780 us -> 662 us (0.85)
  local copies, waits for them, and re-layouts: 125 us -> 4.37 us
  matrix products: 52.7 us -> 79.5 us
  other arithmetic: 24.9 us -> 7.71 us
    reshape x4 -> x0, local copies, waits for them, and re-layouts: 56.7 us -> none  [the longest x1 14.4 us: per_device(): received = received.reshape(experts * capacity, 2 * width)]
    gather x2 -> x0, local copies, waits for them, and re-layouts: 28.6 us -> none  [the longest x1 20.8 us: per_device(): returned[slots].astype(jnp.float32) * combine_w.reshape(-1)[:, None]]
    dot_general x0 -> x4, matrix products: none -> 25.5 us  [the longest x3 20.3 us: per_device(): term = jnp.dot(part, returned, preferred_element_type=jnp.float32)]
    scatter x1 -> x0, local copies, waits for them, and re-layouts: 20 us -> none  [per_device(): jnp.zeros((experts * capacity, 2 * width), jnp.bfloat16).at[slots]]
    convert_element_type x1 -> x0, local copies, waits for them, and re-layouts: 15.5 us -> none  [per_device(): returned[slots].astype(jnp.float32) * combine_w.reshape(-1)[:, None]]
    reduce_sum x1, other arithmetic: 13.9 us -> 0.18 us  [per_device(): spread = jnp.where(hits, combine_w[None, :, :], 0.0).sum(axis=2).T]
where the time goes in v1:
time: 662 us; the launch traced here: 657 us
  blocking collectives  282 us (43%)
  waiting for transfers between devices  279 us (42%)
  matrix products  79.5 us (12%)
  other arithmetic  7.71 us (1%)
    all_to_all x1, blocking collectives, outward(): lax.all_to_all(buffer, ('node', 'local'), split_axis=0, concat_axis=0, ti...  282 us
    all_to_all x1, waiting for transfers between devices, homeward(): lax.all_to_all(buffer, ('node', 'local'), split_axis=0, concat_axis=0, ti...  279 us
    dot_general x3, matrix products, per_device(): term = jnp.dot(part, returned, preferred_element_type=jnp.float32)  20.3 us
  transfers between devices with their start and end apart: 1, of which 1 were waited for; matrix products, arithmetic and copies ran while one was open for 0% of the time, Pallas kernels for 0%

profile of v1, /device:TPU:0, one launch (start us, length us, event | category | flops | bytes accessed | tf_op | source)
XLA Modules:
  0.0 657.1 jit_solution(1001710921023647082)
XLA Ops:
  0.6 0.8 copy.23
  1.7 1.2 reduce-window.6
  2.8 0.2 slice_reduce_fusion
  3.1 0.1 fusion.25
  3.2 0.1 reduce_sum.21
  3.4 0.7 multiply_add_fusion
  4.1 0.2 fusion.17
  4.3 5.2 convolution_convert_fusion
  9.5 281.9 %all_to_all.10 = bf16[32,24,8192]{2,1,0:T(8,128)(2,1)S(1)} all-to-all(bf16[32,24,8192]{2,1,0:T(8,128)(2,1)S(1)} %bitcast.64), channel_id=1, replica_groups=mesh['node'=4,'local'=8] {'node','local'}, dimensions={0} | all-to-all | bytes 25165824 | tf_op jit(solution)/shard_map/all_to_all | solution.py:32
  291.3 9.2 %fusion.10 = f32[768,768]{1,0:T(8,128)} fusion(bf16[1,4096,768]{2,1,0:T(8,128)(2,1)} %param.11, bf16[768,8192]{1,0:T(8,128)(2,1)S(1)} %bitcast.65), kind=kOutput, calls=%fused_computation.16 | convolution fusion | flops 4831838208 | bytes 14942208 | tf_op jit(solution)/shard_map/dot_general | solution.py:10
  300.6 9.4 %fusion.1 = f32[768,768]{1,0:T(8,128)} fusion(bf16[768,8192]{1,0:T(8,128)(2,1)S(1)} %bitcast.66, bf16[1,768,4096]{2,1,0:T(8,128)(2,1)} %param.13), kind=kOutput, calls=%fused_computation.7 | convolution fusion | flops 4831838208 | bytes 14942208 | tf_op jit(solution)/shard_map/dot_general | solution.py:16
  310.0 7.4 %fusion.6 = f32[768,768]{1,0:T(8,128)S(1)} fusion(bf16[1,4096,768]{2,1,0:T(8,128)(2,1)} %param.12, bf16[768,8192]{1,0:T(8,128)(2,1)S(1)} %bitcast.67), kind=kOutput, calls=%fused_computation.12 | convolution fusion | flops 4831838208 | bytes 14942208 | tf_op jit(solution)/shard_map/dot_general | solution.py:11
  317.4 1.4 copy-done.4
  318.8 5.4 convolution_convert_fusion.1
  324.2 12.2 %fusion.8 = f32[768,4096]{1,0:T(8,128)} fusion(bf16[1,4096,768]{2,1,0:T(8,128)(2,1)} %param.11, f32[768,768]{1,0:T(8,128)S(1)} %copy-done.2, f32[768,768]{1,0:T(8,128)S(1)} %copy-done.3, f32[768,768]{1,0:T(8,128)} %copy-done.4), kind=kOutput, calls=%fused_computation.14 | convolution fusion | flops 4837736448 | bytes 25952256 | tf_op jit(solution)/shard_map/dot_general | solution.py:19
  336.4 10.5 %add_convert_fusion = bf16[768,4096]{1,0:T(8,128)(2,1)S(1)} fusion(f32[768,4096]{1,0:T(8,128)} %fusion.8, bf16[1,4096,768]{2,1,0:T(8,128)(2,1)} %param.12, f32[768,768]{1,0:T(8,128)} %fusion.1, f32[768,768]{1,0:T(8,128)} %fusion.10), kind=kOutput, calls=%fused_computation.2 | convolution fusion | flops 4841668608 | bytes 29884416 | tf_op jit(solution)/shard_map/dot_general | solution.py:20
  346.8 5.3 pad_maximum_fusion
  352.1 3.9 all-to-all-start.1
  356.0 0.2 select_reduce_fusion
  356.2 279.0 %all-to-all-done.1 = bf16[32,24,8192]{2,1,0:T(8,128)(2,1)} async-done(((bf16[32,24,8192]{2,1,0:T(8,128)(2,1)}), bf16[32,24,8192]{2,1,0:T(8,128)(2,1)}, u32[]{:S(2)}, u32[]{:S(2)}) %all-to-all-start.1) | async-done | bytes 12582944 | tf_op jit(solution)/shard_map/all_to_all | solution.py:36
  635.3 6.6 %fusion.33 = f32[128,8192]{1,0:T(8,128)S(1)} fusion(bf16[768,8192]{1,0:T(8,128)(2,1)} %bitcast.8, f32[768,128]{1,0:T(8,128)S(1)} %select_reduce_fusion), kind=kOutput, calls=%fused_computation.52 | convolution fusion | flops 1610612736 | bytes 17170432 | tf_op jit(solution)/shard_map/dot_general | solution.py:67
  641.9 6.9 %convolution_add_fusion.1 = f32[128,8192]{1,0:T(8,128)S(1)} fusion(f32[128,8192]{1,0:T(8,128)S(1)} %fusion.33, bf16[768,8192]{1,0:T(8,128)(2,1)} %bitcast.8, f32[768,128]{1,0:T(8,128)S(1)} %select_reduce_fusion), kind=kOutput, calls=%fused_computation.4 | convolution fusion | flops 1612054528 | bytes 21364736 | tf_op jit(solution)/shard_map/dot_general | solution.py:67
  648.8 6.8 %fusion = bf16[128,8192]{1,0:T(8,128)(2,1)S(1)} fusion(f32[128,8192]{1,0:T(8,128)S(1)} %convolution_add_fusion.1, bf16[768,8192]{1,0:T(8,128)(2,1)} %bitcast.8, f32[768,128]{1,0:T(8,128)S(1)} %select_reduce_fusion), kind=kOutput, calls=%fused_computation.5 | convolution fusion | flops 1613398016 | bytes 19267584 | tf_op jit(solution)/shard_map/dot_general | solution.py:67
  655.6 1.5 fusion.32
  (20 shorter events, 0.3 us)
Async XLA Ops:
  300.6 18.2 %slice-start = ((s8[6291456]{0:T(1024)(128)(4,1)}), s8[4194304]{0:T(1024)(128)(4,1)S(1)}, s32[]{:S(2)}) async-start(s8[6291456]{0:T(1024)(128)(4,1)} %bitcast.68), calls=%async_computation.2 | async-start | bytes 8388608
  310.0 8.8 %slice-start.1 = ((s8[6291456]{0:T(1024)(128)(4,1)}), s8[2097152]{0:T(1024)(128)(4,1)S(1)}, s32[]{:S(2)}) async-start(s8[6291456]{0:T(1024)(128)(4,1)} %bitcast.68), calls=%async_computation.3 | async-start | bytes 4194304
  310.0 8.8 %copy-start.1 = (f32[768,768]{1,0:T(8,128)S(1)}, f32[768,768]{1,0:T(8,128)}, u32[]{:S(2)}) copy-start(f32[768,768]{1,0:T(8,128)} %fusion.10) | copy-start | bytes 7077892
  317.4 1.4 copy-start.4
  318.8 5.4 copy-start.2
  318.8 5.4 copy-start.3
  352.1 3.9 copy-start
  352.1 283.1 %all-to-all-start.1 = ((bf16[32,24,8192]{2,1,0:T(8,128)(2,1)}), bf16[32,24,8192]{2,1,0:T(8,128)(2,1)}, u32[]{:S(2)}, u32[]{:S(2)}) async-start(bf16[32,24,8192]{2,1,0:T(8,128)(2,1)} %bitcast.63), calls=%async_computation.1 | async-start | bytes 25165824 | tf_op jit(solution)/shard_map/all_to_all | solution.py:36

commit v2 on v0

--- a/solution.py
+++ b/solution.py
@@ -4,9 +4,7 @@
 from jax.sharding import PartitionSpec as P
 
 
-def expert_rows(rows, gate_w, up_w, down_w, width):
-    inputs = rows[:, :width]
-    upstream = rows[:, width:]
+def expert_rows(inputs, upstream, gate_w, up_w, down_w):
     gate = jnp.dot(inputs, gate_w, preferred_element_type=jnp.float32)
     lifted = jnp.dot(inputs, up_w, preferred_element_type=jnp.float32)
     sigma = jax.nn.sigmoid(gate)
@@ -18,7 +16,7 @@
     d_lift = (back * gate * sigma).astype(jnp.bfloat16)
     grads = lax.dot_general(d_gate, gate_w, contract, preferred_element_type=jnp.float32)
     grads = grads + lax.dot_general(d_lift, up_w, contract, preferred_element_type=jnp.float32)
-    return jnp.concatenate([result, grads.astype(jnp.bfloat16)], axis=1)
+    return jnp.stack([result, grads.astype(jnp.bfloat16)], axis=1)
 
 
 def row_slots(expert_ids, experts, capacity):
@@ -36,23 +34,41 @@
     return lax.all_to_all(buffer, ("node", "local"), split_axis=0, concat_axis=0, tiled=True)
 
 
+def split_three(weights):
+    high = lax.reduce_precision(weights, exponent_bits=8, mantissa_bits=7)
+    rest = weights - high
+    middle = lax.reduce_precision(rest, exponent_bits=8, mantissa_bits=7)
+    low = rest - middle
+    return [part.astype(jnp.bfloat16) for part in (high, middle, low)]
+
+
 def per_device(tokens, grad_out, expert_ids, combine_w, w_gate, w_up, w_down):
     token_count, width = tokens.shape
     top_count = expert_ids.shape[1]
     experts = lax.axis_size("node") * lax.axis_size("local")
     capacity = max(2, (5 * token_count * top_count + 4 * experts - 1) // (4 * experts))
-    slots = row_slots(expert_ids, experts, capacity)
-    owners = jnp.arange(token_count * top_count, dtype=jnp.int32) // top_count
-    paired = jnp.concatenate([tokens, grad_out], axis=1)
-    buffer = jnp.zeros((experts * capacity, 2 * width), jnp.bfloat16).at[slots].set(paired[owners])
-    received = outward(buffer.reshape(experts, capacity, 2 * width))
-    received = received.reshape(experts * capacity, 2 * width)
-    produced = expert_rows(received, w_gate[0], w_up[0], w_down[0], width)
-    returned = homeward(produced.reshape(experts, capacity, 2 * width))
-    returned = returned.reshape(experts * capacity, 2 * width)
-    picked = returned[slots].astype(jnp.float32) * combine_w.reshape(-1)[:, None]
-    summed = jnp.sum(picked.reshape(token_count, top_count, 2 * width), axis=1)
-    return (summed[:, :width].astype(jnp.bfloat16), summed[:, width:].astype(jnp.bfloat16))
+    slots_per = (capacity + 3) // 4 * 4
+    total_slots = experts * slots_per
+    slots = row_slots(expert_ids, experts, slots_per).reshape(token_count, top_count)
+    hits = slots[None, :, :] == jnp.arange(total_slots, dtype=jnp.int32)[:, None, None]
+    taken = jnp.any(hits, axis=2).astype(jnp.bfloat16)
+    blank = jnp.zeros_like(taken)
+    dispatch = jnp.stack([jnp.concatenate([taken, blank], axis=1), jnp.concatenate([blank, taken], axis=1)], axis=1)
+    dispatch = dispatch.reshape(2 * total_slots, 2 * token_count)
+    stacked = jnp.concatenate([tokens, grad_out], axis=0)
+    buffer = jnp.dot(dispatch, stacked, preferred_element_type=jnp.float32).astype(jnp.bfloat16)
+    received = outward(buffer.reshape(experts, 2 * slots_per, width))
+    received = received.reshape(total_slots, 2, width)
+    produced = expert_rows(received[:, 0, :], received[:, 1, :], w_gate[0], w_up[0], w_down[0])
+    returned = homeward(produced.reshape(experts, 2 * slots_per, width))
+    returned = returned.reshape(2 * total_slots, width)
+    spread = jnp.where(hits, combine_w[None, :, :], 0.0).sum(axis=2).T
+    zero = jnp.zeros_like(spread)
+    weights = jnp.concatenate([jnp.stack([spread, zero], axis=2), jnp.stack([zero, spread], axis=2)], axis=0)
+    weights = weights.reshape(2 * token_count, 2 * total_slots)
+    summed = jnp.dot(jnp.concatenate(split_three(weights), axis=0), returned, preferred_element_type=jnp.float32)
+    summed = summed.reshape(3, 2 * token_count, width).sum(axis=0)
+    return (summed[:token_count].astype(jnp.bfloat16), summed[token_count:].astype(jnp.bfloat16))
 
 
 def solution(mesh):

time: 780 us -> 657 us (0.84)
  waiting for transfers between devices: 279 us -> 227 us
  blocking collectives: 282 us -> 237 us
  local copies, waits for them, and re-layouts: 125 us -> 85.7 us
  matrix products: 52.7 us -> 83.2 us
  other arithmetic: 24.9 us -> 12 us
    all_to_all x1, waiting for transfers between devices: 279 us -> 227 us  [homeward(): lax.all_to_all(buffer, ('node', 'local'), split_axis=0, concat_axis=0, ti...]
    all_to_all x1, blocking collectives: 282 us -> 237 us  [outward(): lax.all_to_all(buffer, ('node', 'local'), split_axis=0, concat_axis=0, ti...]
    gather x2 -> x0, local copies, waits for them, and re-layouts: 28.6 us -> none  [the longest x1 20.8 us: per_device(): returned[slots].astype(jnp.float32) * combine_w.reshape(-1)[:, None]]
    slice x2 -> x3, local copies, waits for them, and re-layouts: 1.67 us -> 25.2 us  [the longest x1 23.4 us: per_device(): received[:, 1, :]]
    reshape x4, local copies, waits for them, and re-layouts: 56.7 us -> 34.5 us  [the longest x1 17.3 us: per_device(): received = received.reshape(total_slots, 2, width)]
    another operation x1 -> x4, local copies, waits for them, and re-layouts: 0.01 us -> 20.8 us  [the longest x1 20 us: expert_rows(): return jnp.stack([result, grads.astype(jnp.bfloat16)], axis=1)]
    scatter x1 -> x0, local copies, waits for them, and re-layouts: 20 us -> none  [per_device(): jnp.zeros((experts * capacity, 2 * width), jnp.bfloat16).at[slots]]
    convert_element_type x1 -> x0, local copies, waits for them, and re-layouts: 15.5 us -> none  [per_device(): returned[slots].astype(jnp.float32) * combine_w.reshape(-1)[:, None]]
  transfers between devices with their start and end apart: 1 -> 1, of which waited for: 1 -> 1; matrix products, arithmetic and copies ran while one was open for 0% -> 1% of each run, Pallas kernels for 0% -> 0%
where the time goes in v2:
time: 657 us; the launch traced here: 650 us
  blocking collectives  237 us (36%)
  waiting for transfers between devices  227 us (35%)
  local copies, waits for them, and re-layouts  85.7 us (13%)
  matrix products  83.2 us (13%)
  other arithmetic  12 us (2%)
    all_to_all x1, blocking collectives, outward(): lax.all_to_all(buffer, ('node', 'local'), split_axis=0, concat_axis=0, ti...  237 us
    all_to_all x1, waiting for transfers between devices, homeward(): lax.all_to_all(buffer, ('node', 'local'), split_axis=0, concat_axis=0, ti...  227 us
    slice x1, local copies, waits for them, and re-layouts, per_device(): received[:, 1, :]  23.4 us
    another operation x1, local copies, waits for them, and re-layouts, expert_rows(): return jnp.stack([result, grads.astype(jnp.bfloat16)], axis=1)  20 us
    reshape x1, local copies, waits for them, and re-layouts, per_device(): received = received.reshape(total_slots, 2, width)  17.3 us
    reshape x1, local copies, waits for them, and re-layouts, per_device(): returned = homeward(produced.reshape(experts, 2 * slots_per, width))  16 us
    dot_general x1, matrix products, expert_rows(): gate = jnp.dot(inputs, gate_w, preferred_element_type=jnp.float32)  15.9 us
    dot_general x1, matrix products, expert_rows(): lifted = jnp.dot(inputs, up_w, preferred_element_type=jnp.float32)  13.2 us
  transfers between devices with their start and end apart: 1, of which 1 were waited for; matrix products, arithmetic and copies ran while one was open for 1% of the time, Pallas kernels for 0%

profile of v2, /device:TPU:0, one launch (start us, length us, event | category | flops | bytes accessed | tf_op | source)
XLA Modules:
  0.0 649.8 jit_solution(6033508744405267192)
XLA Ops:
  0.6 0.8 copy.42
  1.7 1.2 reduce-window.6
  3.4 0.7 multiply_add_fusion
  4.5 0.7 copy.49
  5.9 3.1 convolution_convert_fusion
  9.0 237.0 %all_to_all.10 = bf16[32,40,4096]{2,1,0:T(8,128)(2,1)} all-to-all(bf16[32,40,4096]{2,1,0:T(8,128)(2,1)S(1)} %bitcast.62), channel_id=1, replica_groups=mesh['node'=4,'local'=8] {'node','local'}, dimensions={0} | all-to-all | bytes 20971520 | tf_op jit(solution)/shard_map/all_to_all | solution.py:30
  246.0 17.3 %reshape.55 = bf16[640,2,4096]{2,1,0:T(2,128)(2,1)} reshape(bf16[32,40,4096]{2,1,0:T(8,128)(2,1)} %all_to_all.10) | data formatting | bytes 20971520 | tf_op jit(solution)/shard_map/reshape | solution.py:61
  263.3 23.4 %fusion.37 = (bf16[640,1,4096]{2,1,0:T(2,128)(2,1)S(1)}, bf16[640,1,4096]{2,1,0:T(2,128)(2,1)}) fusion(bf16[640,2,4096]{2,1,0:T(2,128)(2,1)} %reshape.55), kind=kLoop, calls=%fused_computation.61 | loop fusion | bytes 20971520 | tf_op jit(solution)/shard_map/slice | solution.py:62
  286.8 15.9 %fusion.8 = f32[640,768]{1,0:T(8,128)} fusion(bf16[1,4096,768]{2,1,0:T(8,128)(2,1)} %param.11, bf16[640,1,4096]{2,1,0:T(2,128)(2,1)} %get-tuple-element.3), kind=kOutput, calls=%fused_computation.12 | convolution fusion | flops 4026531840 | bytes 13500416 | tf_op jit(solution)/shard_map/dot_general | solution.py:8
  302.7 13.2 %fusion.4 = f32[640,768]{1,0:T(8,128)} fusion(bf16[1,4096,768]{2,1,0:T(8,128)(2,1)} %param.12, bf16[640,1,4096]{2,1,0:T(2,128)(2,1)S(1)} %copy-done), kind=kOutput, calls=%fused_computation.8 | convolution fusion | flops 4026531840 | bytes 13500416 | tf_op jit(solution)/shard_map/dot_general | solution.py:9
  315.8 10.5 %fusion = f32[640,768]{1,0:T(8,128)} fusion(bf16[1,768,4096]{2,1,0:T(8,128)(2,1)S(1)} %bitcast.67, bf16[640,1,4096]{2,1,0:T(2,128)(2,1)S(1)} %get-tuple-element.2), kind=kOutput, calls=%fused_computation.4 | convolution fusion | flops 4026531840 | bytes 13500416 | tf_op jit(solution)/shard_map/dot_general | solution.py:14
  326.4 8.5 %fusion.13 = bf16[640,1,4096]{2,0,1:T(8,128)(2,1)} fusion(bf16[1,768,4096]{2,1,0:T(8,128)(2,1)S(1)} %bitcast.67, f32[640,768]{1,0:T(8,128)} %fusion.4, f32[640,768]{1,0:T(8,128)} %fusion.8), kind=kOutput, calls=%fused_computation.15 | convolution fusion | flops 4032102400 | bytes 15466496 | tf_op jit(solution)/shard_map/dot_general | solution.py:12
  334.9 10.0 %fusion.6 = f32[640,4096]{1,0:T(8,128)} fusion(bf16[1,4096,768]{2,1,0:T(8,128)(2,1)} %param.11, f32[640,768]{1,0:T(8,128)S(1)} %copy-done.4, f32[640,768]{1,0:T(8,128)S(1)} %copy-done.6, f32[640,768]{1,0:T(8,128)S(1)} %copy-done.5), kind=kOutput, calls=%fused_computation.10 | convolution fusion | flops 4031447040 | bytes 22675456 | tf_op jit(solution)/shard_map/dot_general | solution.py:17
  344.9 9.9 %fusion.10 = bf16[640,1,4096]{2,0,1:T(8,128)(2,1)} fusion(f32[640,4096]{1,0:T(8,128)} %fusion.6, bf16[1,4096,768]{2,1,0:T(8,128)(2,1)S(1)} %bitcast.69, f32[640,768]{1,0:T(8,128)} %fusion, f32[640,768]{1,0:T(8,128)} %fusion.8), kind=kOutput, calls=%fused_computation.14 | convolution fusion | flops 4034723840 | bytes 25952256 | tf_op jit(solution)/shard_map/dot_general | solution.py:18
  354.9 9.0 %pad_maximum_fusion = bf16[640,2,4096]{2,0,1:T(8,128)(2,1)} fusion(bf16[640,1,4096]{2,0,1:T(8,128)(2,1)} %fusion.10, bf16[640,1,4096]{2,0,1:T(8,128)(2,1)} %fusion.13), kind=kLoop, calls=%fused_computation.1 | loop fusion | flops 5242880 | bytes 20971520 | tf_op jit(solution)/shard_map/stack | solution.py:19
  363.9 20.0 %copy.50 = bf16[640,2,4096]{2,1,0:T(2,128)(2,1)} copy(bf16[640,2,4096]{2,0,1:T(8,128)(2,1)} %pad_maximum_fusion) | data formatting | bytes 20971520 | tf_op jit(solution)/shard_map/stack | solution.py:19
  383.9 16.0 %reshape.56 = bf16[32,40,4096]{2,1,0:T(8,128)(2,1)} reshape(bf16[640,2,4096]{2,1,0:T(2,128)(2,1)} %copy.50) | data formatting | bytes 20971520 | tf_op jit(solution)/shard_map/reshape | solution.py:63
  399.9 4.1 all-to-all-start.1
  404.4 1.1 copy.47
  405.5 0.9 reshape.52
  406.9 2.3 copy.48
  409.2 226.8 %all-to-all-done.1 = bf16[32,40,4096]{2,1,0:T(8,128)(2,1)} async-done(((bf16[32,40,4096]{2,1,0:T(8,128)(2,1)}), bf16[32,40,4096]{2,1,0:T(8,128)(2,1)}, u32[]{:S(2)}, u32[]{:S(2)}) %all-to-all-start.1) | async-done | bytes 10485792 | tf_op jit(solution)/shard_map/all_to_all | solution.py:34
  636.0 12.0 %convolution_reduce_fusion = bf16[256,4096]{1,0:T(8,128)(2,1)S(1)} fusion(bf16[3,256,1280]{2,1,0:T(8,128)(2,1)} %bitcast.63, bf16[1280,4096,1]{1,0,2:T(8,128)(2,1)} %bitcast.13), kind=kOutput, calls=%fused_computation.20 | convolution fusion | flops 8055160832 | bytes 14548992 | tf_op jit(solution)/shard_map/dot_general | solution.py:69
  648.1 1.5 fusion.38
  (43 shorter events, 2.7 us)
Async XLA Ops:
  4.4 1.2 copy-start.1
  4.4 1.5 copy-start.2
  286.8 15.9 %copy-start = (bf16[640,1,4096]{2,1,0:T(2,128)(2,1)S(1)}, bf16[640,1,4096]{2,1,0:T(2,128)(2,1)}, u32[]{:S(2)}) copy-start(bf16[640,1,4096]{2,1,0:T(2,128)(2,1)} %get-tuple-element.3) | copy-start | bytes 15728644
  286.8 29.1 %slice-start = ((s8[6291456]{0:T(1024)(128)(4,1)}), s8[4194304]{0:T(1024)(128)(4,1)S(1)}, s32[]{:S(2)}) async-start(s8[6291456]{0:T(1024)(128)(4,1)} %bitcast.66), calls=%async_computation.2 | async-start | bytes 8388608
  302.7 13.2 %slice-start.1 = ((s8[6291456]{0:T(1024)(128)(4,1)}), s8[2097152]{0:T(1024)(128)(4,1)S(1)}, s32[]{:S(2)}) async-start(s8[6291456]{0:T(1024)(128)(4,1)} %bitcast.66), calls=%async_computation.3 | async-start | bytes 4194304
  326.4 8.5 %copy-start.4 = (f32[640,768]{1,0:T(8,128)S(1)}, f32[640,768]{1,0:T(8,128)}, u32[]{:S(2)}) copy-start(f32[640,768]{1,0:T(8,128)} %fusion.8) | copy-start | bytes 5898244
  326.4 8.5 %copy-start.5 = (f32[640,768]{1,0:T(8,128)S(1)}, f32[640,768]{1,0:T(8,128)}, u32[]{:S(2)}) copy-start(f32[640,768]{1,0:T(8,128)} %fusion.4) | copy-start | bytes 5898244
  326.4 8.5 %copy-start.6 = (f32[640,768]{1,0:T(8,128)S(1)}, f32[640,768]{1,0:T(8,128)}, u32[]{:S(2)}) copy-start(f32[640,768]{1,0:T(8,128)} %fusion) | copy-start | bytes 5898244
  326.4 18.6 %slice-start.2 = ((s8[6291456]{0:T(1024)(128)(4,1)}), s8[2097152]{0:T(1024)(128)(4,1)S(1)}, s32[]{:S(2)}) async-start(s8[6291456]{0:T(1024)(128)(4,1)} %bitcast.68), calls=%async_computation.4 | async-start | bytes 4194304
  334.9 10.1 %slice-start.3 = ((s8[6291456]{0:T(1024)(128)(4,1)}), s8[4194304]{0:T(1024)(128)(4,1)S(1)}, s32[]{:S(2)}) async-start(s8[6291456]{0:T(1024)(128)(4,1)} %bitcast.68), calls=%async_computation.5 | async-start | bytes 8388608
  399.9 4.1 copy-start.3
  399.9 236.1 %all-to-all-start.1 = ((bf16[32,40,4096]{2,1,0:T(8,128)(2,1)}), bf16[32,40,4096]{2,1,0:T(8,128)(2,1)}, u32[]{:S(2)}, u32[]{:S(2)}) async-start(bf16[32,40,4096]{2,1,0:T(8,128)(2,1)} %reshape.56), calls=%async_computation.1 | async-start | bytes 20971520 | tf_op jit(solution)/shard_map/all_to_all | solution.py:34

commit v3 on v2

--- a/solution.py
+++ b/solution.py
@@ -16,7 +16,7 @@
     d_lift = (back * gate * sigma).astype(jnp.bfloat16)
     grads = lax.dot_general(d_gate, gate_w, contract, preferred_element_type=jnp.float32)
     grads = grads + lax.dot_general(d_lift, up_w, contract, preferred_element_type=jnp.float32)
-    return jnp.stack([result, grads.astype(jnp.bfloat16)], axis=1)
+    return result, grads.astype(jnp.bfloat16)
 
 
 def row_slots(expert_ids, experts, capacity):
@@ -48,24 +48,40 @@
     experts = lax.axis_size("node") * lax.axis_size("local")
     capacity = max(2, (5 * token_count * top_count + 4 * experts - 1) // (4 * experts))
     slots_per = (capacity + 3) // 4 * 4
-    total_slots = experts * slots_per
+    main = slots_per // 8 * 8
+    tail = slots_per - main
+    chunk = 2 * slots_per
     slots = row_slots(expert_ids, experts, slots_per).reshape(token_count, top_count)
-    hits = slots[None, :, :] == jnp.arange(total_slots, dtype=jnp.int32)[:, None, None]
+    place = jnp.arange(chunk, dtype=jnp.int32)
+    in_tail = place >= 2 * main
+    rank = jnp.where(in_tail, main + (place - 2 * main) % jnp.maximum(tail, 1), place % jnp.maximum(main, 1))
+    part = jnp.where(in_tail, (place - 2 * main) // jnp.maximum(tail, 1), place // jnp.maximum(main, 1))
+    row_slot = (jnp.arange(experts, dtype=jnp.int32)[:, None] * slots_per + rank[None, :]).reshape(-1)
+    row_part = jnp.tile(part, experts)
+    hits = slots[None, :, :] == row_slot[:, None, None]
     taken = jnp.any(hits, axis=2).astype(jnp.bfloat16)
     blank = jnp.zeros_like(taken)
-    dispatch = jnp.stack([jnp.concatenate([taken, blank], axis=1), jnp.concatenate([blank, taken], axis=1)], axis=1)
-    dispatch = dispatch.reshape(2 * total_slots, 2 * token_count)
+    first = (row_part == 0)[:, None]
+    dispatch = jnp.concatenate([jnp.where(first, taken, blank), jnp.where(first, blank, taken)], axis=1)
     stacked = jnp.concatenate([tokens, grad_out], axis=0)
     buffer = jnp.dot(dispatch, stacked, preferred_element_type=jnp.float32).astype(jnp.bfloat16)
-    received = outward(buffer.reshape(experts, 2 * slots_per, width))
-    received = received.reshape(total_slots, 2, width)
-    produced = expert_rows(received[:, 0, :], received[:, 1, :], w_gate[0], w_up[0], w_down[0])
-    returned = homeward(produced.reshape(experts, 2 * slots_per, width))
-    returned = returned.reshape(2 * total_slots, width)
+    received = outward(buffer.reshape(experts, chunk, width))
+    inputs = received[:, :main].reshape(experts * main, width)
+    upstream = received[:, main:2 * main].reshape(experts * main, width)
+    if tail:
+        ends = received[:, 2 * main:].reshape(experts, 2, tail, width)
+        inputs = jnp.concatenate([inputs, ends[:, 0].reshape(experts * tail, width)], axis=0)
+        upstream = jnp.concatenate([upstream, ends[:, 1].reshape(experts * tail, width)], axis=0)
+    result, grads = expert_rows(inputs, upstream, w_gate[0], w_up[0], w_down[0])
+    pieces = [result[:experts * main].reshape(experts, main, width), grads[:experts * main].reshape(experts, main, width)]
+    if tail:
+        pieces += [result[experts * main:].reshape(experts, tail, width), grads[experts * main:].reshape(experts, tail, width)]
+    produced = jnp.concatenate(pieces, axis=1)
+    returned = homeward(produced).reshape(experts * chunk, width)
     spread = jnp.where(hits, combine_w[None, :, :], 0.0).sum(axis=2).T
     zero = jnp.zeros_like(spread)
-    weights = jnp.concatenate([jnp.stack([spread, zero], axis=2), jnp.stack([zero, spread], axis=2)], axis=0)
-    weights = weights.reshape(2 * token_count, 2 * total_slots)
+    first = (row_part == 0)[None, :]
+    weights = jnp.concatenate([jnp.where(first, spread, zero), jnp.where(first, zero, spread)], axis=0)
     summed = jnp.dot(jnp.concatenate(split_three(weights), axis=0), returned, preferred_element_type=jnp.float32)
     summed = summed.reshape(3, 2 * token_count, width).sum(axis=0)
     return (summed[:token_count].astype(jnp.bfloat16), summed[token_count:].astype(jnp.bfloat16))

time: 657 us -> 583 us (0.89)
  local copies, waits for them, and re-layouts: 85.7 us -> 31.2 us
  matrix products: 83.2 us -> 64.8 us
    reshape x4 -> x3, local copies, waits for them, and re-layouts: 34.5 us -> 4.6 us  [the longest x1 2.73 us: per_device(): ends = received[:, 2 * main:].reshape(experts, 2, tail, width)]
    another operation x4, local copies, waits for them, and re-layouts: 20.8 us -> 1.63 us  [the longest x1 1.34 us: per_device(): ends[:, 0].reshape(experts * tail, width)]
    concatenate x1, other arithmetic: 0.09 us -> 9.88 us  [per_device(): produced = jnp.concatenate(pieces, axis=1)]
    another operation x4 -> x2, other arithmetic: 10.3 us -> 1.2 us  [the longest x1 8.99 us: expert_rows(): return jnp.stack([result, grads.astype(jnp.bfloat16)], axis=1)]
    dot_general x1, matrix products: 15.9 us -> 7.19 us  [expert_rows(): gate = jnp.dot(inputs, gate_w, preferred_element_type=jnp.float32)]
    slice x2 -> x9, local copies, waits for them, and re-layouts: 23.7 us -> 15.8 us  [the longest x1 4.75 us: per_device(): grads[:experts * main].reshape(experts, main, width)]
    dot_general x1, matrix products: 13.2 us -> 5.56 us  [expert_rows(): lifted = jnp.dot(inputs, up_w, preferred_element_type=jnp.float32)]
where the time goes in v3:
time: 583 us; the launch traced here: 580 us
  blocking collectives  237 us (41%)
  waiting for transfers between devices  229 us (39%)
  matrix products  64.8 us (11%)
  local copies, waits for them, and re-layouts  31.2 us (5%)
  other arithmetic  13.6 us (2%)
    all_to_all x1, blocking collectives, outward(): lax.all_to_all(buffer, ('node', 'local'), split_axis=0, concat_axis=0, ti...  237 us
    all_to_all x1, waiting for transfers between devices, homeward(): lax.all_to_all(buffer, ('node', 'local'), split_axis=0, concat_axis=0, ti...  229 us
    dot_general x1, matrix products, expert_rows(): lax.dot_general(d_lift, up_w, contract, preferred_element_type=jnp.float32)  13.5 us
    dot_general x1, matrix products, per_device(): jnp.dot(jnp.concatenate(split_three(weights), axis=0), returned, preferre...  12 us
  transfers between devices with their start and end apart: 1, of which 1 were waited for; matrix products, arithmetic and copies ran while one was open for 1% of the time, Pallas kernels for 0%

profile of v3, /device:TPU:0, one launch (start us, length us, event | category | flops | bytes accessed | tf_op | source)
XLA Modules:
  0.0 580.3 jit_solution(17637125741548657842)
XLA Ops:
  1.7 1.2 reduce-window.6
  5.0 4.7 convolution_convert_fusion
  9.7 236.9 %all_to_all.10 = bf16[32,40,4096]{2,1,0:T(8,128)(2,1)S(1)} all-to-all(bf16[32,40,4096]{2,1,0:T(8,128)(2,1)S(1)} %bitcast.45), channel_id=1, replica_groups=mesh['node'=4,'local'=8] {'node','local'}, dimensions={0} | all-to-all | bytes 20971520 | tf_op jit(solution)/shard_map/all_to_all | solution.py:30
  246.6 4.0 copy-done
  250.6 1.4 slice.56
  252.0 2.7 reshape.150
  254.7 2.2 fusion.41
  256.9 1.3 reshape_squeeze.6
  258.6 3.9 fusion.39
  262.5 7.2 %fusion.8 = f32[640,768]{1,0:T(8,128)S(1)} fusion(bf16[1,4096,768]{2,1,0:T(8,128)(2,1)} %param.11, bf16[128,4096]{1,0:T(8,128)(2,1)S(1)} %reshape_squeeze.6, bf16[512,4096]{1,0:T(8,128)(2,1)S(1)} %bitcast.49), kind=kOutput, calls=%fused_computation.12 | convolution fusion | flops 4037017600 | bytes 13500416 | tf_op jit(solution)/shard_map/dot_general | solution.py:8
  269.8 5.6 fusion.4
  275.4 5.6 fusion
  281.0 6.3 %convolution_convert_fusion.1 = bf16[640,4096]{1,0:T(8,128)(2,1)S(1)} fusion(bf16[1,768,4096]{2,1,0:T(8,128)(2,1)S(1)} %bitcast.53, f32[640,768]{1,0:T(8,128)} %fusion.4, f32[640,768]{1,0:T(8,128)S(1)} %fusion.8), kind=kOutput, calls=%fused_computation.3 | convolution fusion | flops 4032102400 | bytes 15466496 | tf_op jit(solution)/shard_map/dot_general | solution.py:12
  287.3 9.8 %fusion.6 = f32[640,4096]{1,0:T(8,128)} fusion(bf16[1,4096,768]{2,1,0:T(8,128)(2,1)} %param.11, f32[640,768]{1,0:T(8,128)S(1)} %fusion.8, f32[640,768]{1,0:T(8,128)S(1)} %copy-done.4, f32[640,768]{1,0:T(8,128)S(1)} %copy-done.3), kind=kOutput, calls=%fused_computation.10 | convolution fusion | flops 4031447040 | bytes 22675456 | tf_op jit(solution)/shard_map/dot_general | solution.py:17
  297.2 13.5 %add_convert_fusion = bf16[640,4096]{1,0:T(8,128)(2,1)} fusion(f32[640,4096]{1,0:T(8,128)} %fusion.6, bf16[1,4096,768]{2,1,0:T(8,128)(2,1)} %param.12, f32[640,768]{1,0:T(8,128)} %fusion, f32[640,768]{1,0:T(8,128)} %copy-done.2), kind=kOutput, calls=%fused_computation.2 | convolution fusion | flops 4034723840 | bytes 25952256 | tf_op jit(solution)/shard_map/dot_general | solution.py:18
  310.7 4.7 slice.61
  316.5 2.2 slice.58
  319.1 1.5 reshape.154
  320.6 9.9 %pad_maximum_fusion = bf16[32,40,4096]{2,1,0:T(8,128)(2,1)} fusion(bf16[32,4,4096]{2,1,0:T(4,128)(2,1)S(1)} %reshape.155, bf16[32,4,4096]{2,1,0:T(4,128)(2,1)S(1)} %reshape.154, bf16[32,16,4096]{2,1,0:T(8,128)(2,1)} %bitcast.46, bf16[32,16,4096]{2,1,0:T(8,128)(2,1)} %bitcast.47), kind=kLoop, calls=%fused_computation.1 | loop fusion | flops 41943040 | bytes 20971520 | tf_op jit(solution)/shard_map/concatenate | solution.py:79
  330.5 4.1 all-to-all-start.1
  335.7 2.3 copy.28
  338.0 228.7 %all-to-all-done.1 = bf16[32,40,4096]{2,1,0:T(8,128)(2,1)} async-done(((bf16[32,40,4096]{2,1,0:T(8,128)(2,1)}), bf16[32,40,4096]{2,1,0:T(8,128)(2,1)}, u32[]{:S(2)}, u32[]{:S(2)}) %all-to-all-start.1) | async-done | bytes 10485792 | tf_op jit(solution)/shard_map/all_to_all | solution.py:34
  566.7 12.0 %convolution_reduce_fusion = bf16[256,4096]{1,0:T(8,128)(2,1)S(1)} fusion(bf16[3,256,1280]{2,1,0:T(8,128)(2,1)} %bitcast.51, bf16[1280,4096,1]{1,0,2:T(8,128)(2,1)} %bitcast.13), kind=kOutput, calls=%fused_computation.20 | convolution fusion | flops 8055160832 | bytes 14548992 | tf_op jit(solution)/shard_map/dot_general | solution.py:85
  578.7 1.5 fusion.40
  (48 shorter events, 5.9 us)
Async XLA Ops:
  246.6 4.0 copy-start
  258.5 11.2 %slice-start.3 = ((s8[6291456]{0:T(1024)(128)(4,1)}), s8[4194304]{0:T(1024)(128)(4,1)S(1)}, s32[]{:S(2)}) async-start(s8[6291456]{0:T(1024)(128)(4,1)} %bitcast.54), calls=%async_computation.5 | async-start | bytes 8388608
  262.5 7.2 %slice-start.4 = ((s8[6291456]{0:T(1024)(128)(4,1)}), s8[2097152]{0:T(1024)(128)(4,1)S(1)}, s32[]{:S(2)}) async-start(s8[6291456]{0:T(1024)(128)(4,1)} %bitcast.54), calls=%async_computation.6 | async-start | bytes 4194304
  262.5 12.8 %slice-start.1 = ((s8[6291456]{0:T(1024)(128)(4,1)}), s8[4194304]{0:T(1024)(128)(4,1)S(1)}, s32[]{:S(2)}) async-start(s8[6291456]{0:T(1024)(128)(4,1)} %bitcast.52), calls=%async_computation.3 | async-start | bytes 8388608
  269.8 17.5 %copy-start.2 = (f32[640,768]{1,0:T(8,128)}, f32[640,768]{1,0:T(8,128)S(1)}, u32[]{:S(2)}) copy-start(f32[640,768]{1,0:T(8,128)S(1)} %fusion.8) | copy-start | bytes 5898244
  269.8 5.6 slice-start.2
  281.0 6.3 %copy-start.3 = (f32[640,768]{1,0:T(8,128)S(1)}, f32[640,768]{1,0:T(8,128)}, u32[]{:S(2)}) copy-start(f32[640,768]{1,0:T(8,128)} %fusion.4) | copy-start | bytes 5898244
  281.0 6.3 %copy-start.4 = (f32[640,768]{1,0:T(8,128)S(1)}, f32[640,768]{1,0:T(8,128)}, u32[]{:S(2)}) copy-start(f32[640,768]{1,0:T(8,128)} %fusion) | copy-start | bytes 5898244
  316.5 2.2 slice-start
  330.5 4.2 copy-start.1
  330.5 236.2 %all-to-all-start.1 = ((bf16[32,40,4096]{2,1,0:T(8,128)(2,1)}), bf16[32,40,4096]{2,1,0:T(8,128)(2,1)}, u32[]{:S(2)}, u32[]{:S(2)}) async-start(bf16[32,40,4096]{2,1,0:T(8,128)(2,1)} %pad_maximum_fusion), calls=%async_computation.1 | async-start | bytes 20971520 | tf_op jit(solution)/shard_map/all_to_all | solution.py:34

commit v4 on v2

v4 whole, which is shorter than its diff:
```python
import jax
import jax.numpy as jnp
from jax import lax
from jax.sharding import PartitionSpec as P


def expert_rows(inputs, upstream, gate_w, up_w, down_w):
    gate = jnp.dot(inputs, gate_w, preferred_element_type=jnp.float32)
    lifted = jnp.dot(inputs, up_w, preferred_element_type=jnp.float32)
    sigma = jax.nn.sigmoid(gate)
    active = (gate * sigma * lifted).astype(jnp.bfloat16)
    result = jnp.dot(active, down_w, preferred_element_type=jnp.float32).astype(jnp.bfloat16)
    contract = (((1,), (1,)), ((), ()))
    back = lax.dot_general(upstream, down_w, contract, preferred_element_type=jnp.float32)
    d_gate = (back * lifted * sigma * (1.0 + gate * (1.0 - sigma))).astype(jnp.bfloat16)
    d_lift = (back * gate * sigma).astype(jnp.bfloat16)
    grads = lax.dot_general(d_gate, gate_w, contract, preferred_element_type=jnp.float32)
    grads = grads + lax.dot_general(d_lift, up_w, contract, preferred_element_type=jnp.float32)
    return result, grads.astype(jnp.bfloat16)


def row_slots(expert_ids, experts, capacity):
    flat_ids = expert_ids.reshape(-1)
    onehot = (flat_ids[:, None] == jnp.arange(experts, dtype=jnp.int32)[None, :]).astype(jnp.int32)
    ranks = jnp.sum((jnp.cumsum(onehot, axis=0) - 1) * onehot, axis=1)
    return flat_ids * capacity + ranks


def inward(buffer):
    return lax.all_to_all(buffer, ("node", "sub"), split_axis=0, concat_axis=0, tiled=True)


def split_three(weights):
    high = lax.reduce_precision(weights, exponent_bits=8, mantissa_bits=7)
    rest = weights - high
    middle = lax.reduce_precision(rest, exponent_bits=8, mantissa_bits=7)
    low = rest - middle
    return [part.astype(jnp.bfloat16) for part in (high, middle, low)]


def per_device(tokens, grad_out, expert_ids, combine_w, w_gate, w_up, w_down):
    token_count, width = tokens.shape
    top_count = expert_ids.shape[1]
    halves = lax.axis_size("half")
    subs = lax.axis_size("sub")
    group_size = lax.axis_size("node") * subs
    experts = group_size * halves
    capacity = max(2, (5 * token_count * top_count + 4 * experts - 1) // (4 * experts))
    slots_per = (2 * capacity + 7) // 8 * 8
    total_slots = group_size * slots_per
    swap = [(i, (i + 1) % halves) for i in range(halves)]
    stacked = jnp.concatenate([tokens, grad_out], axis=0)
    far_stacked = lax.ppermute(stacked, "half", swap)
    ids = jnp.concatenate([expert_ids, lax.ppermute(expert_ids, "half", swap)], axis=0)
    wts = jnp.concatenate([combine_w, lax.ppermute(combine_w, "half", swap)], axis=0)
    near = (ids % (halves * subs)) // subs == lax.axis_index("half")
    group = (ids // (halves * subs)) * subs + ids % subs
    flat = jnp.where(near, group, group_size).reshape(-1)
    onehot = (flat[:, None] == jnp.arange(group_size, dtype=jnp.int32)[None, :]).astype(jnp.int32)
    ranks = jnp.sum((jnp.cumsum(onehot, axis=0) - 1) * onehot, axis=1)
    slots = jnp.where(flat < group_size, flat * slots_per + ranks, -1).reshape(2 * token_count, top_count)
    hits = slots[None, :, :] == jnp.arange(total_slots, dtype=jnp.int32)[:, None, None]
    taken = jnp.any(hits, axis=2).astype(jnp.bfloat16).reshape(group_size, 1, slots_per, 2 * token_count)
    blank = jnp.zeros_like(taken)
    dispatch = jnp.concatenate([jnp.concatenate([taken, blank], axis=3), jnp.concatenate([blank, taken], axis=3)], axis=1)
    dispatch = dispatch.reshape(2 * total_slots, 4 * token_count)
    source = jnp.concatenate([tokens, far_stacked[:token_count], grad_out, far_stacked[token_count:]], axis=0)
    buffer = jnp.dot(dispatch, source, preferred_element_type=jnp.float32).astype(jnp.bfloat16)
    received = inward(buffer.reshape(group_size, 2 * slots_per, width))
    inputs = received[:, :slots_per].reshape(total_slots, width)
    upstream = received[:, slots_per:].reshape(total_slots, width)
    result, grads = expert_rows(inputs, upstream, w_gate[0], w_up[0], w_down[0])
    produced = jnp.concatenate([result.reshape(group_size, slots_per, width), grads.reshape(group_size, slots_per, width)], axis=1)
    returned = inward(produced)
    spread = jnp.where(hits, wts[None, :, :], 0.0).sum(axis=2).T
    parts = jnp.concatenate(split_three(spread), axis=0)
    mixed = jnp.dot(parts, returned[:, :slots_per].reshape(total_slots, width), preferred_element_type=jnp.float32)
    grad_in = jnp.dot(parts, returned[:, slots_per:].reshape(total_slots, width), preferred_element_type=jnp.float32)
    mixed = mixed.reshape(3, 2 * token_count, width).sum(axis=0)
    grad_in = grad_in.reshape(3, 2 * token_count, width).sum(axis=0)
    far_part = jnp.concatenate([mixed[token_count:], grad_in[token_count:]], axis=0).astype(jnp.bfloat16)
    near_part = lax.ppermute(far_part, "half", swap).astype(jnp.float32)
    mixed = mixed[:token_count] + near_part[:token_count]
    grad_in = grad_in[:token_count] + near_part[token_count:]
    return (mixed.astype(jnp.bfloat16), grad_in.astype(jnp.bfloat16))


def solution(mesh):
    nodes = mesh.shape["node"]
    locals_ = mesh.shape["local"]
    grid = jax.sharding.Mesh(mesh.devices.reshape(nodes, 2, locals_ // 2), ("node", "half", "sub"))
    rows = P(("node", "half", "sub"), None)
    stack = P(("node", "half", "sub"), None, None)
    return jax.shard_map(
        per_device,
        mesh=grid,
        in_specs=(rows, rows, rows, rows, stack, stack, stack),
        out_specs=(rows, rows),
        check_vma=False,
    )
```

time: 657 us -> 552 us (0.84); the launches traced: 650 us -> 552 us
  blocking collectives: 237 us -> 121 us
  waiting for transfers between devices: 227 us -> 305 us
  local copies, waits for them, and re-layouts: 85.7 us -> 21.7 us
  matrix products: 83.2 us -> 66.5 us
  starting transfers between devices: 4.05 us -> 16.1 us
  other arithmetic: 12 us -> 20.6 us
    ppermute x0 -> x4, waiting for transfers between devices: none -> 303 us  [the longest x1 122 us: per_device(): lax.ppermute(combine_w, 'half', swap)]
    all_to_all x1, waiting for transfers between devices: 227 us -> 1.66 us  [inward(): lax.all_to_all(buffer, ('node', 'sub'), split_axis=0, concat_axis=0, tile...]
    all_to_all x1, blocking collectives: 237 us -> 121 us  [inward(): lax.all_to_all(buffer, ('node', 'sub'), split_axis=0, concat_axis=0, tile...]
    reshape x4 -> x0, local copies, waits for them, and re-layouts: 34.5 us -> none  [the longest x1 17.3 us: per_device(): received = received.reshape(total_slots, 2, width)]
    another operation x4 -> x2, local copies, waits for them, and re-layouts: 20.8 us -> 0.08 us  [the longest x1 20 us: expert_rows(): return jnp.stack([result, grads.astype(jnp.bfloat16)], axis=1)]
    concatenate x2 -> x7, other arithmetic: 0.22 us -> 12.2 us  [the longest x1 8.7 us: per_device(): jnp.concatenate([result.reshape(group_size, slots_per, width), grads.resh...]
    ppermute x0 -> x4, starting transfers between devices: none -> 10.9 us  [the longest x1 4.04 us: per_device(): far_stacked = lax.ppermute(stacked, 'half', swap)]
    dot_general x1, matrix products: 15.9 us -> 8.13 us  [expert_rows(): gate = jnp.dot(inputs, gate_w, preferred_element_type=jnp.float32)]
  transfers between devices with their start and end apart: 1 -> 5, of which waited for: 1 -> 4; matrix products, arithmetic and copies ran while one was open for 1% -> 1% of each run, Pallas kernels for 0% -> 0%
where the time goes in v4:
time: 552 us
  waiting for transfers between devices  305 us (55%)
  blocking collectives  121 us (22%)
  matrix products  66.5 us (12%)
  local copies, waits for them, and re-layouts  21.7 us (4%)
  other arithmetic  20.6 us (4%)
  starting transfers between devices  16.1 us (3%)
    ppermute x1, waiting for transfers between devices, per_device(): lax.ppermute(combine_w, 'half', swap)  122 us
    all_to_all x1, blocking collectives, inward(): lax.all_to_all(buffer, ('node', 'sub'), split_axis=0, concat_axis=0, tile...  121 us
    ppermute x1, waiting for transfers between devices, per_device(): lax.ppermute(expert_ids, 'half', swap)  90.8 us
    ppermute x1, waiting for transfers between devices, per_device(): near_part = lax.ppermute(far_part, 'half', swap).astype(jnp.float32)  90.4 us
    dot_general x1, matrix products, expert_rows(): lax.dot_general(d_lift, up_w, contract, preferred_element_type=jnp.float32)  13.6 us
  transfers between devices with their start and end apart: 5, of which 4 were waited for; matrix products, arithmetic and copies ran while one was open for 1% of the time, Pallas kernels for 0%

profile of v4, /device:TPU:0, one launch (start us, length us, event | category | flops | bytes accessed | tf_op | source)
XLA Modules:
  0.0 551.5 jit_solution(3001000497488908443)
XLA Ops:
  0.6 3.1 pad_maximum_fusion.1
  3.7 4.0 collective-permute-start.2
  7.9 90.8 %collective-permute-done = s32[128,4]{0,1:T(4,128)S(1)} collective-permute-done((s32[128,4]{0,1:T(4,128)S(1)}, s32[128,4]{0,1:T(4,128)S(1)}, u32[]{:S(2)}, u32[]{:S(2)}) %collective-permute-start) | collective-permute-done | bytes 2080 | tf_op jit(solution)/shard_map/ppermute | solution.py:54
  99.1 4.5 reduce-window.6
  105.8 5.8 %convolution_convert_fusion = bf16[1280,4096]{1,0:T(8,128)(2,1)S(1)} fusion(bf16[1280,512]{1,0:T(8,128)(2,1)S(1)} %bitcast.71, bf16[128,4096]{1,0:T(8,128)(2,1)S(1)} %get-tuple-element.9, bf16[128,4096]{1,0:T(8,128)(2,1)S(1)} %copy-done.2, bf16[128,4096]{1,0:T(8,128)(2,1)S(1)} %get-tuple-element.8, bf16[128,4096]{1,0:T(8,128)(2,1)S(1)} %copy-done.3), kind=kOutput, calls=%fused_computation | convolution fusion | flops 5390729216 | bytes 15990784 | tf_op jit(solution)/shard_map/dot_general | solution.py:68
  111.6 120.8 %all_to_all.10 = bf16[16,80,4096]{2,1,0:T(8,128)(2,1)} all-to-all(bf16[16,80,4096]{2,1,0:T(8,128)(2,1)S(1)} %bitcast.61), channel_id=1, replica_groups=mesh['node'=4,'half'=2,'sub'=4] {'node','sub'}, dimensions={0} | all-to-all | bytes 20971520 | tf_op jit(solution)/shard_map/all_to_all | solution.py:30
  232.4 9.8 %fusion.62 = (bf16[16,40,4096]{2,1,0:T(8,128)(2,1)}, bf16[16,40,4096]{2,1,0:T(8,128)(2,1)}) fusion(bf16[16,80,4096]{2,1,0:T(8,128)(2,1)} %all_to_all.10), kind=kLoop, calls=%fused_computation.133 | loop fusion | bytes 20971520 | tf_op jit(solution)/shard_map/slice | solution.py:71
  242.3 8.1 %fusion.8 = f32[640,768]{1,0:T(8,128)S(1)} fusion(bf16[640,4096]{1,0:T(8,128)(2,1)} %bitcast.67, bf16[1,4096,768]{2,1,0:T(8,128)(2,1)} %param.11), kind=kOutput, calls=%fused_computation.12 | convolution fusion | flops 4026531840 | bytes 13500416 | tf_op jit(solution)/shard_map/dot_general | solution.py:8
  250.5 5.5 fusion.4
  256.0 5.6 %fusion = f32[640,768]{1,0:T(8,128)} fusion(bf16[640,4096]{1,0:T(8,128)(2,1)S(1)} %bitcast.66, bf16[1,768,4096]{2,1,0:T(8,128)(2,1)S(1)} %bitcast.78), kind=kOutput, calls=%fused_computation.4 | convolution fusion | flops 4026531840 | bytes 13500416 | tf_op jit(solution)/shard_map/dot_general | solution.py:14
  261.7 4.5 convolution_convert_fusion.1
  266.2 9.7 %fusion.6 = f32[640,4096]{1,0:T(8,128)} fusion(bf16[1,4096,768]{2,1,0:T(8,128)(2,1)S(1)} %bitcast.80, f32[640,768]{1,0:T(8,128)S(1)} %fusion.8, f32[640,768]{1,0:T(8,128)} %fusion, f32[640,768]{1,0:T(8,128)S(1)} %copy-done.7), kind=kOutput, calls=%fused_computation.10 | convolution fusion | flops 4031447040 | bytes 22675456 | tf_op jit(solution)/shard_map/dot_general | solution.py:17
  275.9 13.6 %add_convert_fusion = bf16[640,4096]{1,0:T(8,128)(2,1)} fusion(f32[640,4096]{1,0:T(8,128)} %fusion.6, bf16[1,4096,768]{2,1,0:T(8,128)(2,1)} %param.12, f32[640,768]{1,0:T(8,128)} %fusion, f32[640,768]{1,0:T(8,128)} %copy-done.6), kind=kOutput, calls=%fused_computation.2 | convolution fusion | flops 4034723840 | bytes 25952256 | tf_op jit(solution)/shard_map/dot_general | solution.py:18
  289.4 8.7 %pad_maximum_fusion = bf16[16,80,4096]{2,1,0:T(8,128)(2,1)} fusion(bf16[16,40,4096]{2,1,0:T(8,128)(2,1)} %bitcast.69, bf16[16,40,4096]{2,1,0:T(8,128)(2,1)S(1)} %bitcast.62), kind=kLoop, calls=%fused_computation.1 | loop fusion | flops 20971520 | bytes 20971520 | tf_op jit(solution)/shard_map/concatenate | solution.py:73
  298.1 5.2 all-to-all-start.1
  303.4 3.4 collective-permute-start.1
  306.8 121.9 %collective-permute-done.1 = f32[128,4]{0,1:T(4,128)S(1)} collective-permute-done((f32[128,4]{0,1:T(4,128)S(1)}, f32[128,4]{0,1:T(4,128)S(1)}, u32[]{:S(2)}, u32[]{:S(2)}) %collective-permute-start.1) | collective-permute-done | bytes 2080 | tf_op jit(solution)/shard_map/ppermute | solution.py:55
  430.0 1.7 all-to-all-done.1
  431.6 9.5 %fusion.61 = (bf16[16,40,4096]{2,1,0:T(8,128)(2,1)}, bf16[16,40,4096]{2,1,0:T(8,128)(2,1)}) fusion(bf16[16,80,4096]{2,1,0:T(8,128)(2,1)} %all-to-all-done.1), kind=kLoop, calls=%fused_computation.132 | loop fusion | bytes 20971520 | tf_op jit(solution)/shard_map/slice | solution.py:77
  441.2 8.2 %convolution_reduce_fusion.1 = f32[256,4096]{1,0:T(8,128)S(1)} fusion(bf16[3,256,640]{2,1,0:T(8,128)(2,1)S(1)} %bitcast.73, bf16[640,4096,1]{1,0,2:T(8,128)(2,1)} %bitcast.70), kind=kOutput, calls=%fused_computation.22 | convolution fusion | flops 4028628992 | bytes 10420224 | tf_op jit(solution)/shard_map/dot_general | solution.py:77
  449.5 5.6 %convolution_reduce_fusion = f32[256,4096]{1,0:T(8,128)S(1)} fusion(bf16[3,256,640]{2,1,0:T(8,128)(2,1)S(1)} %bitcast.74, bf16[640,4096,1]{1,0,2:T(8,128)(2,1)S(1)} %bitcast.63), kind=kOutput, calls=%fused_computation.21 | convolution fusion | flops 4028628992 | bytes 10420224 | tf_op jit(solution)/shard_map/dot_general | solution.py:78
  455.5 3.4 collective-permute-start.3
  458.8 90.4 %collective-permute-done.3 = bf16[256,4096]{1,0:T(8,128)(2,1)S(1)} collective-permute-done((bf16[256,4096]{1,0:T(8,128)(2,1)S(1)}, bf16[256,4096]{1,0:T(8,128)(2,1)S(1)}, u32[]{:S(2)}, u32[]{:S(2)}) %collective-permute-start.3) | collective-permute-done | bytes 2097184 | tf_op jit(solution)/shard_map/ppermute | solution.py:82
  549.7 1.8 fusion.20
  (68 shorter events, 4.8 us)
Async XLA Ops:
  0.6 7.2 %copy-start.4 = (s32[128,4]{0,1:T(4,128)S(1)}, s32[128,4]{0,1:T(4,128)}, u32[]{:S(2)}) copy-start(s32[128,4]{0,1:T(4,128)} %param.9) | copy-start | bytes 6148
  3.7 101.7 %copy-start.2 = (bf16[128,4096]{1,0:T(8,128)(2,1)S(1)}, bf16[128,4096]{1,0:T(8,128)(2,1)}, u32[]{:S(2)}) copy-start(bf16[128,4096]{1,0:T(8,128)(2,1)} %param.8) | copy-start | bytes 3145732
  3.7 101.5 %collective-permute-start.2 = (bf16[256,4096]{1,0:T(8,128)(2,1)}, bf16[256,4096]{1,0:T(8,128)(2,1)S(1)}, u32[]{:S(2)}, u32[]{:S(2)}) collective-permute-start(bf16[256,4096]{1,0:T(8,128)(2,1)} %pad_maximum_fusion.1), channel_id=1, source_target_pairs={{0,4},{4,0},{1,5},{5,1},{2,6},{6,2},{3,7},{7,3},{8,12},{12,8},{9,1... | collective-permute-start | bytes 6291464 | tf_op jit(solution)/shard_map/ppermute | solution.py:53
  7.8 90.9 %collective-permute-start = (s32[128,4]{0,1:T(4,128)S(1)}, s32[128,4]{0,1:T(4,128)S(1)}, u32[]{:S(2)}, u32[]{:S(2)}) collective-permute-start(s32[128,4]{0,1:T(4,128)S(1)} %copy-done.4), channel_id=1, source_target_pairs={{0,4},{4,0},{1,5},{5,1},{2,6},{6,2},{3,7},{7,3},{8,12},{12,8},{9,1... | collective-permute-start | bytes 6152 | tf_op jit(solution)/shard_map/ppermute | solution.py:54
  104.5 1.2 copy-start.3
  232.4 18.0 %slice-start.6 = ((s8[6291456]{0:T(1024)(128)(4,1)}), s8[2097152]{0:T(1024)(128)(4,1)S(1)}, s32[]{:S(2)}) async-start(s8[6291456]{0:T(1024)(128)(4,1)} %bitcast.81), calls=%async_computation.8 | async-start | bytes 4194304
  242.3 8.2 %copy-start.1 = (bf16[16,40,4096]{2,1,0:T(8,128)(2,1)S(1)}, bf16[16,40,4096]{2,1,0:T(8,128)(2,1)}, u32[]{:S(2)}) copy-start(bf16[16,40,4096]{2,1,0:T(8,128)(2,1)} %get-tuple-element.5) | copy-start | bytes 15728644
  242.3 8.2 %slice-start.7 = ((s8[6291456]{0:T(1024)(128)(4,1)}), s8[4194304]{0:T(1024)(128)(4,1)S(1)}, s32[]{:S(2)}) async-start(s8[6291456]{0:T(1024)(128)(4,1)} %bitcast.81), calls=%async_computation.9 | async-start | bytes 8388608
  242.3 13.7 %slice-start = ((s8[5242880]{0:T(1024)(128)(4,1)}), s8[4194304]{0:T(1024)(128)(4,1)S(1)}, s32[]{:S(2)}) async-start(s8[5242880]{0:T(1024)(128)(4,1)} %bitcast.64), calls=%async_computation.2 | async-start | bytes 8388608
  242.3 13.7 %slice-start.2 = ((s8[6291456]{0:T(1024)(128)(4,1)}), s8[4194304]{0:T(1024)(128)(4,1)S(1)}, s32[]{:S(2)}) async-start(s8[6291456]{0:T(1024)(128)(4,1)} %bitcast.77), calls=%async_computation.4 | async-start | bytes 8388608
  250.5 15.7 %copy-start.6 = (f32[640,768]{1,0:T(8,128)}, f32[640,768]{1,0:T(8,128)S(1)}, u32[]{:S(2)}) copy-start(f32[640,768]{1,0:T(8,128)S(1)} %fusion.8) | copy-start | bytes 5898244
  250.5 5.5 %slice-start.1 = ((s8[5242880]{0:T(1024)(128)(4,1)}), s8[1048576]{0:T(1024)(128)(4,1)S(1)}, s32[]{:S(2)}) async-start(s8[5242880]{0:T(1024)(128)(4,1)} %bitcast.64), calls=%async_computation.3 | async-start | bytes 2097152
  250.5 5.5 slice-start.3
  250.5 15.7 %slice-start.4 = ((s8[6291456]{0:T(1024)(128)(4,1)}), s8[4194304]{0:T(1024)(128)(4,1)S(1)}, s32[]{:S(2)}) async-start(s8[6291456]{0:T(1024)(128)(4,1)} %bitcast.79), calls=%async_computation.6 | async-start | bytes 8388608
  256.0 5.7 %copy-start.7 = (f32[640,768]{1,0:T(8,128)S(1)}, f32[640,768]{1,0:T(8,128)}, u32[]{:S(2)}) copy-start(f32[640,768]{1,0:T(8,128)} %fusion.4) | copy-start | bytes 5898244
  256.0 10.2 %slice-start.5 = ((s8[6291456]{0:T(1024)(128)(4,1)}), s8[2097152]{0:T(1024)(128)(4,1)S(1)}, s32[]{:S(2)}) async-start(s8[6291456]{0:T(1024)(128)(4,1)} %bitcast.79), calls=%async_computation.7 | async-start | bytes 4194304
  298.1 5.2 copy-start.5
  298.1 133.5 %all-to-all-start.1 = ((bf16[16,80,4096]{2,1,0:T(8,128)(2,1)}), bf16[16,80,4096]{2,1,0:T(8,128)(2,1)}, u32[]{:S(2)}, u32[]{:S(2)}) async-start(bf16[16,80,4096]{2,1,0:T(8,128)(2,1)} %pad_maximum_fusion), calls=%async_computation.1 | async-start | bytes 20971520 | tf_op jit(solution)/shard_map/all_to_all | solution.py:30
  303.4 125.3 %collective-permute-start.1 = (f32[128,4]{0,1:T(4,128)S(1)}, f32[128,4]{0,1:T(4,128)S(1)}, u32[]{:S(2)}, u32[]{:S(2)}) collective-permute-start(f32[128,4]{0,1:T(4,128)S(1)} %copy-done.5), channel_id=1, source_target_pairs={{0,4},{4,0},{1,5},{5,1},{2,6},{6,2},{3,7},{7,3},{8,12},{12,8},{9,1... | collective-permute-start | bytes 6152 | tf_op jit(solution)/shard_map/ppermute | solution.py:55
  441.2 8.3 %copy-start = (bf16[16,40,4096]{2,1,0:T(8,128)(2,1)S(1)}, bf16[16,40,4096]{2,1,0:T(8,128)(2,1)}, u32[]{:S(2)}) copy-start(bf16[16,40,4096]{2,1,0:T(8,128)(2,1)} %get-tuple-element.3) | copy-start | bytes 15728644
  455.5 93.8 %collective-permute-start.3 = (bf16[256,4096]{1,0:T(8,128)(2,1)S(1)}, bf16[256,4096]{1,0:T(8,128)(2,1)S(1)}, u32[]{:S(2)}, u32[]{:S(2)}) collective-permute-start(bf16[256,4096]{1,0:T(8,128)(2,1)S(1)} %pad_maximum_fusion.2), channel_id=1, source_target_pairs={{0,4},{4,0},{1,5},{5,1},{2,6},{6,2},{3,7},{7,3},{8,12},{12,8},{9,1... | collective-permute-start | bytes 6291464 | tf_op jit(solution)/shard_map/ppermute | solution.py:82

commit v5 on v4

v5 whole, which is shorter than its diff:
```python
import jax
import jax.numpy as jnp
from jax import lax
from jax.sharding import PartitionSpec as P


def expert_rows(inputs, upstream, gate_w, up_w, down_w):
    gate = jnp.dot(inputs, gate_w, preferred_element_type=jnp.float32)
    lifted = jnp.dot(inputs, up_w, preferred_element_type=jnp.float32)
    sigma = jax.nn.sigmoid(gate)
    active = (gate * sigma * lifted).astype(jnp.bfloat16)
    result = jnp.dot(active, down_w, preferred_element_type=jnp.float32).astype(jnp.bfloat16)
    contract = (((1,), (1,)), ((), ()))
    back = lax.dot_general(upstream, down_w, contract, preferred_element_type=jnp.float32)
    d_gate = (back * lifted * sigma * (1.0 + gate * (1.0 - sigma))).astype(jnp.bfloat16)
    d_lift = (back * gate * sigma).astype(jnp.bfloat16)
    grads = lax.dot_general(d_gate, gate_w, contract, preferred_element_type=jnp.float32)
    grads = grads + lax.dot_general(d_lift, up_w, contract, preferred_element_type=jnp.float32)
    return result, grads.astype(jnp.bfloat16)


def row_slots(expert_ids, experts, capacity):
    flat_ids = expert_ids.reshape(-1)
    onehot = (flat_ids[:, None] == jnp.arange(experts, dtype=jnp.int32)[None, :]).astype(jnp.int32)
    ranks = jnp.sum((jnp.cumsum(onehot, axis=0) - 1) * onehot, axis=1)
    return flat_ids * capacity + ranks


def inward(buffer):
    return lax.all_to_all(buffer, ("node", "sub"), split_axis=0, concat_axis=0, tiled=True)


def split_three(weights):
    high = lax.reduce_precision(weights, exponent_bits=8, mantissa_bits=7)
    rest = weights - high
    middle = lax.reduce_precision(rest, exponent_bits=8, mantissa_bits=7)
    low = rest - middle
    return [part.astype(jnp.bfloat16) for part in (high, middle, low)]


def chunk_rows(group_size, slots_per):
    main = slots_per // 8 * 8
    tail = slots_per - main
    place = jnp.arange(2 * slots_per, dtype=jnp.int32)
    in_tail = place >= 2 * main
    rank = jnp.where(in_tail, main + (place - 2 * main) % max(tail, 1), place % max(main, 1))
    part = jnp.where(in_tail, (place - 2 * main) // max(tail, 1), place // max(main, 1))
    row_slot = (jnp.arange(group_size, dtype=jnp.int32)[:, None] * slots_per + rank[None, :]).reshape(-1)
    return row_slot, jnp.tile(part, group_size) == 0


def route(ids, near, group, group_size, slots_per):
    flat = jnp.where(near, group, group_size).reshape(-1)
    onehot = (flat[:, None] == jnp.arange(group_size, dtype=jnp.int32)[None, :]).astype(jnp.int32)
    ranks = jnp.sum((jnp.cumsum(onehot, axis=0) - 1) * onehot, axis=1)
    return jnp.where(flat < group_size, flat * slots_per + ranks, -1).reshape(ids.shape)


def pack(slots, inputs, upstream, row_slot, first):
    hits = slots[None, :, :] == row_slot[:, None, None]
    taken = jnp.any(hits, axis=2).astype(jnp.bfloat16)
    blank = jnp.zeros_like(taken)
    dispatch = jnp.concatenate([jnp.where(first[:, None], taken, blank), jnp.where(first[:, None], blank, taken)], axis=1)
    source = jnp.concatenate([inputs, upstream], axis=0)
    return jnp.dot(dispatch, source, preferred_element_type=jnp.float32).astype(jnp.bfloat16)


def combine(slots, wts, returned, row_slot, first):
    spread = jnp.where(slots[None, :, :] == row_slot[:, None, None], wts[None, :, :], 0.0).sum(axis=2).T
    zero = jnp.zeros_like(spread)
    weights = jnp.concatenate([jnp.where(first[None, :], spread, zero), jnp.where(first[None, :], zero, spread)], axis=0)
    parts = jnp.concatenate(split_three(weights), axis=0)
    summed = jnp.dot(parts, returned, preferred_element_type=jnp.float32)
    return summed.reshape(3, weights.shape[0], returned.shape[1]).sum(axis=0)


def unpack(received, main, tail):
    group_size, _, width = received.shape
    inputs = [received[:, :main].reshape(group_size * main, width)]
    upstream = [received[:, main:2 * main].reshape(group_size * main, width)]
    if tail:
        ends = received[:, 2 * main:].reshape(group_size, 2, tail, width)
        inputs.append(ends[:, 0].reshape(group_size * tail, width))
        upstream.append(ends[:, 1].reshape(group_size * tail, width))
    return inputs, upstream


def repack(result, grads, group_size, main, tail):
    width = result.shape[1]
    edge = group_size * main
    pieces = [result[:edge].reshape(group_size, main, width), grads[:edge].reshape(group_size, main, width)]
    if tail:
        pieces += [result[edge:].reshape(group_size, tail, width), grads[edge:].reshape(group_size, tail, width)]
    return jnp.concatenate(pieces, axis=1)


def per_device(tokens, grad_out, expert_ids, combine_w, w_gate, w_up, w_down):
    token_count, width = tokens.shape
    top_count = expert_ids.shape[1]
    halves = lax.axis_size("half")
    subs = lax.axis_size("sub")
    group_size = lax.axis_size("node") * subs
    experts = group_size * halves
    capacity = max(2, (5 * token_count * top_count + 4 * experts - 1) // (4 * experts))
    slots_per = (capacity + 3) // 4 * 4
    main = slots_per // 8 * 8
    tail = slots_per - main
    row_slot, first = chunk_rows(group_size, slots_per)
    swap = [(i, (i + 1) % halves) for i in range(halves)]
    here = lax.axis_index("half")
    far_stacked = lax.ppermute(jnp.concatenate([tokens, grad_out], axis=0), "half", swap)
    far_ids = lax.ppermute(expert_ids, "half", swap)
    far_w = lax.ppermute(combine_w, "half", swap)

    def near_slots(ids):
        near = (ids % (halves * subs)) // subs == here
        group = (ids // (halves * subs)) * subs + ids % subs
        return route(ids, near, group, group_size, slots_per)

    own_slots = near_slots(expert_ids)
    far_slots = near_slots(far_ids)
    own_sent = inward(pack(own_slots, tokens, grad_out, row_slot, first).reshape(group_size, 2 * slots_per, width))
    far_sent = pack(far_slots, far_stacked[:token_count], far_stacked[token_count:], row_slot, first)
    far_sent = inward(far_sent.reshape(group_size, 2 * slots_per, width))
    own_in, own_up = unpack(own_sent, main, tail)
    far_in, far_up = unpack(far_sent, main, tail)
    result, grads = expert_rows(jnp.concatenate(own_in + far_in, axis=0), jnp.concatenate(own_up + far_up, axis=0),
                                w_gate[0], w_up[0], w_down[0])
    half_rows = group_size * slots_per
    far_back = inward(repack(result[half_rows:], grads[half_rows:], group_size, main, tail))
    far_sum = combine(far_slots, far_w, far_back.reshape(2 * half_rows, width), row_slot, first)
    near_part = lax.ppermute(far_sum.astype(jnp.bfloat16), "half", swap).astype(jnp.float32)
    own_back = inward(repack(result[:half_rows], grads[:half_rows], group_size, main, tail))
    own_sum = combine(own_slots, combine_w, own_back.reshape(2 * half_rows, width), row_slot, first) + near_part
    return (own_sum[:token_count].astype(jnp.bfloat16), own_sum[token_count:].astype(jnp.bfloat16))


def solution(mesh):
    nodes = mesh.shape["node"]
    locals_ = mesh.shape["local"]
    grid = jax.sharding.Mesh(mesh.devices.reshape(nodes, 2, locals_ // 2), ("node", "half", "sub"))
    rows = P(("node", "half", "sub"), None)
    stack = P(("node", "half", "sub"), None, None)
    return jax.shard_map(
        per_device,
        mesh=grid,
        in_specs=(rows, rows, rows, rows, stack, stack, stack),
        out_specs=(rows, rows),
        check_vma=False,
    )
```

time: 552 us -> 525 us (0.951)
  blocking collectives: 121 us -> 0 us
  waiting for transfers between devices: 305 us -> 365 us
  starting transfers between devices: 16.1 us -> 30.5 us
  local copies, waits for them, and re-layouts: 21.7 us -> 35.4 us
  matrix products: 66.5 us -> 74.9 us
    all_to_all x1 -> x0, blocking collectives: 121 us -> none  [inward(): lax.all_to_all(buffer, ('node', 'sub'), split_axis=0, concat_axis=0, tile...]
    all_to_all x1 -> x4, waiting for transfers between devices: 1.66 us -> 116 us  [inward(): lax.all_to_all(buffer, ('node', 'sub'), split_axis=0, concat_axis=0, tile...]
    ppermute x4, waiting for transfers between devices: 303 us -> 249 us  [the longest x1 108 us: per_device(): lax.ppermute(jnp.concatenate([tokens, grad_out], axis=0), 'half', swap)]
    all_to_all x1 -> x4, starting transfers between devices: 5.24 us -> 19.2 us  [inward(): lax.all_to_all(buffer, ('node', 'sub'), split_axis=0, concat_axis=0, tile...]
    dot_general x3 -> x4, matrix products: 19.6 us -> 24.8 us  [the longest x2 17 us: combine(): summed = jnp.dot(parts, returned, preferred_element_type=jnp.float32)]
    slice x7 -> x12, local copies, waits for them, and re-layouts: 20 us -> 22.1 us  [the longest x2 7.55 us: unpack(): upstream = [received[:, main:2 * main].reshape(group_size * main, width)]]
    concatenate x7 -> x4, other arithmetic: 12.2 us -> 11.1 us  [the longest x2 11 us: repack(): return jnp.concatenate(pieces, axis=1)]
  transfers between devices with their start and end apart: 5 -> 8, of which waited for: 4 -> 5; matrix products, arithmetic and copies ran while one was open for 1% -> 8% of each run, Pallas kernels for 0% -> 0%
where the time goes in v5:
time: 525 us
  waiting for transfers between devices  365 us (70%)
  matrix products  74.9 us (14%)
  local copies, waits for them, and re-layouts  35.4 us (7%)
  starting transfers between devices  30.5 us (6%)
  other arithmetic  17.6 us (3%)
    all_to_all x4, waiting for transfers between devices, inward(): lax.all_to_all(buffer, ('node', 'sub'), split_axis=0, concat_axis=0, tile...  116 us
    ppermute x1, waiting for transfers between devices, per_device(): lax.ppermute(jnp.concatenate([tokens, grad_out], axis=0), 'half', swap)  108 us
    ppermute x1, waiting for transfers between devices, per_device(): lax.ppermute(far_sum.astype(jnp.bfloat16), 'half', swap).astype(jnp.float32)  81.9 us
    ppermute x1, waiting for transfers between devices, per_device(): far_w = lax.ppermute(combine_w, 'half', swap)  59.2 us
    all_to_all x4, starting transfers between devices, inward(): lax.all_to_all(buffer, ('node', 'sub'), split_axis=0, concat_axis=0, tile...  19.2 us
    dot_general x2, matrix products, combine(): summed = jnp.dot(parts, returned, preferred_element_type=jnp.float32)  17 us
    dot_general x1, matrix products, expert_rows(): lax.dot_general(d_gate, gate_w, contract, preferred_element_type=jnp.floa...  12.8 us
    dot_general x1, matrix products, expert_rows(): lax.dot_general(d_lift, up_w, contract, preferred_element_type=jnp.float32)  11.2 us
  transfers between devices with their start and end apart: 8, of which 5 were waited for; matrix products, arithmetic and copies ran while one was open for 8% of the time, Pallas kernels for 0%

profile of v5, /device:TPU:0, one launch (start us, length us, event | category | flops | bytes accessed | tf_op | source)
XLA Modules:
  0.0 524.5 jit_solution(10565596623046124355)
XLA Ops:
  1.4 4.1 collective-permute-start
  14.0 3.9 convolution_convert_fusion.2
  18.0 4.9 all-to-all-start
  23.2 107.5 %collective-permute-done.1 = bf16[256,4096]{1,0:T(8,128)(2,1)S(1)} collective-permute-done((bf16[256,4096]{1,0:T(8,128)(2,1)S(1)}, bf16[256,4096]{1,0:T(8,128)(2,1)S(1)}, u32[]{:S(2)}, u32[]{:S(2)}) %collective-permute-start.1) | collective-permute-done | bytes 2097184 | tf_op jit(solution)/shard_map/ppermute | solution.py:111
  130.8 3.9 convolution_convert_fusion.1
  134.6 4.8 all-to-all-start.1
  142.0 4.7 fusion.71
  146.7 57.8 %all-to-all-done.1 = bf16[16,40,4096]{2,1,0:T(8,128)(2,1)} async-done(((bf16[16,40,4096]{2,1,0:T(8,128)(2,1)}), bf16[16,40,4096]{2,1,0:T(8,128)(2,1)}, u32[]{:S(2)}, u32[]{:S(2)}) %all-to-all-start.1) | async-done | bytes 5242912 | tf_op jit(solution)/shard_map/all_to_all | solution.py:30
  210.1 7.2 %fusion.8 = f32[640,768]{1,0:T(8,128)S(1)} fusion(bf16[1,4096,768]{2,1,0:T(8,128)(2,1)} %param.11, bf16[64,4096]{1,0:T(8,128)(2,1)S(1)} %reshape_squeeze.13, bf16[256,4096]{1,0:T(8,128)(2,1)S(1)} %bitcast.89, bf16[64,4096]{1,0:T(8,128)(2,1)S(1)} %reshape_squeeze.12, bf16[256,4096]{1,0:T(8,128)(2,1)S(1)} %bitcast.86), kind=kOutput, calls=%fused_computation.12 | convolution fusion | flops 4047503360 | bytes 13500416 | tf_op jit(solution)/shard_map/dot_general | solution.py:8
  217.3 5.5 %fusion.4 = f32[640,768]{1,0:T(8,128)} fusion(bf16[1,4096,768]{2,1,0:T(8,128)(2,1)S(1)} %bitcast.96, bf16[64,4096]{1,0:T(8,128)(2,1)S(1)} %reshape_squeeze.13, bf16[256,4096]{1,0:T(8,128)(2,1)S(1)} %bitcast.90, bf16[64,4096]{1,0:T(8,128)(2,1)S(1)} %reshape_squeeze.12, bf16[256,4096]{1,0:T(8,128)(2,1)S(1)} %bitcast.87), kind=kOutput, calls=%fused_computation.8 | convolution fusion | flops 4047503360 | bytes 13500416 | tf_op jit(solution)/shard_map/dot_general | solution.py:9
  222.9 7.9 %convolution_convert_fusion = bf16[640,4096]{1,0:T(8,128)(2,1)} fusion(bf16[1,768,4096]{2,1,0:T(8,128)(2,1)S(1)} %bitcast.94, f32[640,768]{1,0:T(8,128)} %fusion.4, f32[640,768]{1,0:T(8,128)S(1)} %fusion.8), kind=kOutput, calls=%fused_computation.1 | convolution fusion | flops 4032102400 | bytes 15466496 | tf_op jit(solution)/shard_map/dot_general | solution.py:12
  230.7 5.5 %fusion = f32[640,768]{1,0:T(8,128)} fusion(bf16[1,768,4096]{2,1,0:T(8,128)(2,1)S(1)} %bitcast.94, bf16[64,4096]{1,0:T(8,128)(2,1)S(1)} %reshape_squeeze.15, bf16[256,4096]{1,0:T(8,128)(2,1)S(1)} %bitcast.88, bf16[64,4096]{1,0:T(8,128)(2,1)S(1)} %reshape_squeeze.14, bf16[256,4096]{1,0:T(8,128)(2,1)S(1)} %bitcast.85), kind=kOutput, calls=%fused_computation.4 | convolution fusion | flops 4047503360 | bytes 13500416 | tf_op jit(solution)/shard_map/dot_general | solution.py:14
  236.3 12.8 %fusion.6 = f32[640,4096]{1,0:T(8,128)} fusion(bf16[1,4096,768]{2,1,0:T(8,128)(2,1)} %param.11, f32[640,768]{1,0:T(8,128)S(1)} %fusion.8, f32[640,768]{1,0:T(8,128)} %fusion, f32[640,768]{1,0:T(8,128)} %fusion.4), kind=kOutput, calls=%fused_computation.10 | convolution fusion | flops 4031447040 | bytes 22675456 | tf_op jit(solution)/shard_map/dot_general | solution.py:17
  249.1 11.2 %add_convert_fusion = bf16[640,4096]{1,0:T(8,128)(2,1)S(1)} fusion(f32[640,4096]{1,0:T(8,128)} %fusion.6, bf16[1,4096,768]{2,1,0:T(8,128)(2,1)} %param.12, f32[640,768]{1,0:T(8,128)} %fusion, f32[640,768]{1,0:T(8,128)} %copy-done.7), kind=kOutput, calls=%fused_computation | convolution fusion | flops 4034723840 | bytes 25952256 | tf_op jit(solution)/shard_map/dot_general | solution.py:18
  263.5 4.5 fusion.68
  273.0 5.9 %pad_maximum_fusion.2 = bf16[16,40,4096]{2,1,0:T(8,128)(2,1)} fusion(bf16[16,4,4096]{2,1,0:T(4,128)(2,1)S(1)} %reshape.225, bf16[16,4,4096]{2,1,0:T(4,128)(2,1)S(1)} %reshape.224, bf16[16,16,4096]{2,1,0:T(8,128)(2,1)} %bitcast.81, bf16[16,16,4096]{2,1,0:T(8,128)(2,1)} %bitcast.82), kind=kLoop, calls=%fused_computation.23 | loop fusion | flops 20971520 | bytes 10485760 | tf_op jit(solution)/shard_map/concatenate | solution.py:94
  279.0 5.0 all-to-all-start.3
  285.4 5.0 pad_maximum_fusion.1
  290.4 58.5 %all-to-all-done.3 = bf16[16,40,4096]{2,1,0:T(8,128)(2,1)} async-done(((bf16[16,40,4096]{2,1,0:T(8,128)(2,1)}), bf16[16,40,4096]{2,1,0:T(8,128)(2,1)}, u32[]{:S(2)}, u32[]{:S(2)}) %all-to-all-start.3) | async-done | bytes 5242912 | tf_op jit(solution)/shard_map/all_to_all | solution.py:30
  349.0 4.6 all-to-all-start.2
  357.0 59.2 %collective-permute-done.2 = f32[128,4]{0,1:T(4,128)S(1)} collective-permute-done((f32[128,4]{0,1:T(4,128)S(1)}, f32[128,4]{0,1:T(4,128)S(1)}, u32[]{:S(2)}, u32[]{:S(2)}) %collective-permute-start.2) | collective-permute-done | bytes 2080 | tf_op jit(solution)/shard_map/ppermute | solution.py:113
  418.7 9.5 %convolution_reduce_fusion = bf16[256,4096]{1,0:T(8,128)(2,1)} fusion(bf16[3,256,640]{2,1,0:T(8,128)(2,1)S(1)} %bitcast.92, bf16[640,4096,1]{1,0,2:T(8,128)(2,1)} %bitcast.24), kind=kOutput, calls=%fused_computation.25 | convolution fusion | flops 4028628992 | bytes 8323072 | tf_op jit(solution)/shard_map/dot_general | solution.py:73
  432.8 7.5 %convolution_reduce_fusion.1 = f32[256,4096]{1,0:T(8,128)S(1)} fusion(bf16[3,256,640]{2,1,0:T(8,128)(2,1)} %bitcast.91, bf16[640,4096,1]{1,0,2:T(8,128)(2,1)} %bitcast.17), kind=kOutput, calls=%fused_computation.26 | convolution fusion | flops 4028628992 | bytes 10420224 | tf_op jit(solution)/shard_map/dot_general | solution.py:73
  440.4 81.9 %collective-permute-done.3 = bf16[256,4096]{1,0:T(8,128)(2,1)S(1)} collective-permute-done((bf16[256,4096]{1,0:T(8,128)(2,1)}, bf16[256,4096]{1,0:T(8,128)(2,1)S(1)}, u32[]{:S(2)}, u32[]{:S(2)}) %collective-permute-start.3) | collective-permute-done | bytes 2097184 | tf_op jit(solution)/shard_map/ppermute | solution.py:132
  (102 shorter events, 40.0 us)
Async XLA Ops:
  1.4 9.9 %collective-permute-start = (s32[128,4]{1,0:T(8,128)S(1)}, s32[128,4]{1,0:T(8,128)S(1)}, u32[]{:S(2)}, u32[]{:S(2)}) collective-permute-start(s32[128,4]{1,0:T(8,128)S(1)} %copy.27), channel_id=1, source_target_pairs={{0,4},{4,0},{1,5},{5,1},{2,6},{6,2},{3,7},{7,3},{8,12},{12,8},{9,1... | collective-permute-start | bytes 6152 | tf_op jit(solution)/shard_map/ppermute | solution.py:112
  18.0 116.7 %all-to-all-start = ((bf16[16,40,4096]{2,1,0:T(8,128)(2,1)}), bf16[16,40,4096]{2,1,0:T(8,128)(2,1)}, u32[]{:S(2)}, u32[]{:S(2)}) async-start(bf16[16,40,4096]{2,1,0:T(8,128)(2,1)} %bitcast.78), calls=%async_computation | async-start | bytes 10485760 | tf_op jit(solution)/shard_map/all_to_all | solution.py:30
  22.8 107.9 %collective-permute-start.1 = (bf16[256,4096]{1,0:T(8,128)(2,1)S(1)}, bf16[256,4096]{1,0:T(8,128)(2,1)S(1)}, u32[]{:S(2)}, u32[]{:S(2)}) collective-permute-start(bf16[256,4096]{1,0:T(8,128)(2,1)S(1)} %constant_dynamic-update-slice_fusion), channel_id=1, source_target_pairs={{0,4},{4,0},{1,5},{5,1},{2,6},{6,2},{3,7},{7,3},{8,12},{12,8},{9,1... | collective-permute-start | bytes 6291464 | tf_op jit(solution)/shard_map/ppermute | solution.py:111
  134.6 69.9 %all-to-all-start.1 = ((bf16[16,40,4096]{2,1,0:T(8,128)(2,1)}), bf16[16,40,4096]{2,1,0:T(8,128)(2,1)}, u32[]{:S(2)}, u32[]{:S(2)}) async-start(bf16[16,40,4096]{2,1,0:T(8,128)(2,1)} %bitcast.77), calls=%async_computation.1 | async-start | bytes 10485760 | tf_op jit(solution)/shard_map/all_to_all | solution.py:30
  207.1 2.9 copy-start.3
  207.2 10.1 %slice-start.4 = ((s8[6291456]{0:T(1024)(128)(4,1)}), s8[4194304]{0:T(1024)(128)(4,1)S(1)}, s32[]{:S(2)}) async-start(s8[6291456]{0:T(1024)(128)(4,1)} %bitcast.95), calls=%async_computation.8 | async-start | bytes 8388608
  210.1 7.2 %slice-start.5 = ((s8[6291456]{0:T(1024)(128)(4,1)}), s8[2097152]{0:T(1024)(128)(4,1)S(1)}, s32[]{:S(2)}) async-start(s8[6291456]{0:T(1024)(128)(4,1)} %bitcast.95), calls=%async_computation.9 | async-start | bytes 4194304
  210.1 12.8 %slice-start.2 = ((s8[6291456]{0:T(1024)(128)(4,1)}), s8[4194304]{0:T(1024)(128)(4,1)S(1)}, s32[]{:S(2)}) async-start(s8[6291456]{0:T(1024)(128)(4,1)} %bitcast.93), calls=%async_computation.6 | async-start | bytes 8388608
  217.3 19.0 %copy-start.7 = (f32[640,768]{1,0:T(8,128)}, f32[640,768]{1,0:T(8,128)S(1)}, u32[]{:S(2)}) copy-start(f32[640,768]{1,0:T(8,128)S(1)} %fusion.8) | copy-start | bytes 5898244
  217.3 5.5 %slice-start.3 = ((s8[6291456]{0:T(1024)(128)(4,1)}), s8[2097152]{0:T(1024)(128)(4,1)S(1)}, s32[]{:S(2)}) async-start(s8[6291456]{0:T(1024)(128)(4,1)} %bitcast.93), calls=%async_computation.7 | async-start | bytes 4194304
  222.9 7.9 %copy-start.2 = (bf16[16,16,4096]{2,1,0:T(8,128)(2,1)S(1)}, bf16[16,16,4096]{2,1,0:T(8,128)(2,1)}, u32[]{:S(2)}) copy-start(bf16[16,16,4096]{2,1,0:T(8,128)(2,1)} %get-tuple-element.14) | copy-start | bytes 6291460
  260.3 2.3 copy-start
  262.6 5.3 %slice-start = ((s8[5242880]{0:T(1024)(128)(4,1)}), s8[4194304]{0:T(1024)(128)(4,1)S(1)}, s32[]{:S(2)}) async-start(s8[5242880]{0:T(1024)(128)(4,1)} %bitcast.83), calls=%async_computation.4 | async-start | bytes 8388608
  263.5 4.5 slice-start.1
  279.0 5.0 copy-start.1
  279.0 70.0 %all-to-all-start.3 = ((bf16[16,40,4096]{2,1,0:T(8,128)(2,1)}), bf16[16,40,4096]{2,1,0:T(8,128)(2,1)}, u32[]{:S(2)}, u32[]{:S(2)}) async-start(bf16[16,40,4096]{2,1,0:T(8,128)(2,1)} %pad_maximum_fusion.2), calls=%async_computation.3 | async-start | bytes 10485760 | tf_op jit(solution)/shard_map/all_to_all | solution.py:30
  290.4 63.2 %copy-start.6 = (f32[128,4]{0,1:T(4,128)S(1)}, f32[128,4]{0,1:T(4,128)}, u32[]{:S(2)}) copy-start(f32[128,4]{0,1:T(4,128)} %param.10) | copy-start | bytes 6148
  349.0 83.9 %all-to-all-start.2 = ((bf16[16,40,4096]{2,1,0:T(8,128)(2,1)}), bf16[16,40,4096]{2,1,0:T(8,128)(2,1)}, u32[]{:S(2)}, u32[]{:S(2)}) async-start(bf16[16,40,4096]{2,1,0:T(8,128)(2,1)} %pad_maximum_fusion.1), calls=%async_computation.2 | async-start | bytes 10485760 | tf_op jit(solution)/shard_map/all_to_all | solution.py:30
  353.6 62.7 %collective-permute-start.2 = (f32[128,4]{0,1:T(4,128)S(1)}, f32[128,4]{0,1:T(4,128)S(1)}, u32[]{:S(2)}, u32[]{:S(2)}) collective-permute-start(f32[128,4]{0,1:T(4,128)S(1)} %copy-done.6), channel_id=1, source_target_pairs={{0,4},{4,0},{1,5},{5,1},{2,6},{6,2},{3,7},{7,3},{8,12},{12,8},{9,1... | collective-permute-start | bytes 6152 | tf_op jit(solution)/shard_map/ppermute | solution.py:113
  418.6 12.8 %copy-start.4 = (bf16[256,640]{0,1:T(8,128)(2,1)S(1)}, bf16[256,640]{0,1:T(8,128)(2,1)}, u32[]{:S(2)}) copy-start(bf16[256,640]{0,1:T(8,128)(2,1)} %get-tuple-element.43) | copy-start | bytes 983044
  418.6 12.8 %copy-start.5 = (bf16[256,640]{0,1:T(8,128)(2,1)S(1)}, bf16[256,640]{0,1:T(8,128)(2,1)}, u32[]{:S(2)}) copy-start(bf16[256,640]{0,1:T(8,128)(2,1)} %get-tuple-element.44) | copy-start | bytes 983044
  428.1 94.2 %collective-permute-start.3 = (bf16[256,4096]{1,0:T(8,128)(2,1)}, bf16[256,4096]{1,0:T(8,128)(2,1)S(1)}, u32[]{:S(2)}, u32[]{:S(2)}) collective-permute-start(bf16[256,4096]{1,0:T(8,128)(2,1)} %convolution_reduce_fusion), channel_id=1, source_target_pairs={{0,4},{4,0},{1,5},{5,1},{2,6},{6,2},{3,7},{7,3},{8,12},{12,8},{9,1... | collective-permute-start | bytes 6291464 | tf_op jit(solution)/shard_map/ppermute | solution.py:132

commit v6 on v5

--- a/solution.py
+++ b/solution.py
@@ -94,6 +94,29 @@
     return jnp.concatenate(pieces, axis=1)
 
 
+def expert_split(inputs, upstream, gate_w, up_w, down_w):
+    bounds = []
+    edge = 0
+    for piece in inputs:
+        bounds.append((edge, edge + piece.shape[1]))
+        edge += piece.shape[1]
+    contract = (((1,), (1,)), ((), ()))
+    gate = sum(jnp.dot(x, gate_w[a:b], preferred_element_type=jnp.float32) for x, (a, b) in zip(inputs, bounds))
+    lifted = sum(jnp.dot(x, up_w[a:b], preferred_element_type=jnp.float32) for x, (a, b) in zip(inputs, bounds))
+    back = sum(lax.dot_general(g, down_w[:, a:b], contract, preferred_element_type=jnp.float32) for g, (a, b) in zip(upstream, bounds))
+    sigma = jax.nn.sigmoid(gate)
+    active = (gate * sigma * lifted).astype(jnp.bfloat16)
+    d_gate = (back * lifted * sigma * (1.0 + gate * (1.0 - sigma))).astype(jnp.bfloat16)
+    d_lift = (back * gate * sigma).astype(jnp.bfloat16)
+    results, grads = [], []
+    for a, b in bounds:
+        results.append(jnp.dot(active, down_w[:, a:b], preferred_element_type=jnp.float32).astype(jnp.bfloat16))
+        total = lax.dot_general(d_gate, gate_w[a:b], contract, preferred_element_type=jnp.float32)
+        total = total + lax.dot_general(d_lift, up_w[a:b], contract, preferred_element_type=jnp.float32)
+        grads.append(total.astype(jnp.bfloat16))
+    return results, grads
+
+
 def per_device(tokens, grad_out, expert_ids, combine_w, w_gate, w_up, w_down):
     token_count, width = tokens.shape
     top_count = expert_ids.shape[1]
@@ -105,10 +128,13 @@
     slots_per = (capacity + 3) // 4 * 4
     main = slots_per // 8 * 8
     tail = slots_per - main
+    half_rows = group_size * slots_per
     row_slot, first = chunk_rows(group_size, slots_per)
     swap = [(i, (i + 1) % halves) for i in range(halves)]
     here = lax.axis_index("half")
-    far_stacked = lax.ppermute(jnp.concatenate([tokens, grad_out], axis=0), "half", swap)
+    cut = width // 2
+    far_lo = lax.ppermute(jnp.concatenate([tokens[:, :cut], grad_out[:, :cut]], axis=0), "half", swap)
+    far_hi = lax.ppermute(jnp.concatenate([tokens[:, cut:], grad_out[:, cut:]], axis=0), "half", swap)
     far_ids = lax.ppermute(expert_ids, "half", swap)
     far_w = lax.ppermute(combine_w, "half", swap)
 
@@ -120,17 +146,33 @@
     own_slots = near_slots(expert_ids)
     far_slots = near_slots(far_ids)
     own_sent = inward(pack(own_slots, tokens, grad_out, row_slot, first).reshape(group_size, 2 * slots_per, width))
-    far_sent = pack(far_slots, far_stacked[:token_count], far_stacked[token_count:], row_slot, first)
-    far_sent = inward(far_sent.reshape(group_size, 2 * slots_per, width))
+    far_lo, far_w, own_sent = lax.optimization_barrier((far_lo, far_w, own_sent))
+    lo_sent = pack(far_slots, far_lo[:token_count], far_lo[token_count:], row_slot, first)
+    lo_sent = inward(lo_sent.reshape(group_size, 2 * slots_per, cut))
+    far_hi, lo_sent = lax.optimization_barrier((far_hi, lo_sent))
+    hi_sent = pack(far_slots, far_hi[:token_count], far_hi[token_count:], row_slot, first)
+    hi_sent = inward(hi_sent.reshape(group_size, 2 * slots_per, width - cut))
     own_in, own_up = unpack(own_sent, main, tail)
-    far_in, far_up = unpack(far_sent, main, tail)
-    result, grads = expert_rows(jnp.concatenate(own_in + far_in, axis=0), jnp.concatenate(own_up + far_up, axis=0),
-                                w_gate[0], w_up[0], w_down[0])
-    half_rows = group_size * slots_per
-    far_back = inward(repack(result[half_rows:], grads[half_rows:], group_size, main, tail))
-    far_sum = combine(far_slots, far_w, far_back.reshape(2 * half_rows, width), row_slot, first)
-    near_part = lax.ppermute(far_sum.astype(jnp.bfloat16), "half", swap).astype(jnp.float32)
-    own_back = inward(repack(result[:half_rows], grads[:half_rows], group_size, main, tail))
+    own_res, own_grads = expert_split([jnp.concatenate(own_in, axis=0)], [jnp.concatenate(own_up, axis=0)],
+                                      w_gate[0], w_up[0], w_down[0])
+    own_packed = repack(own_res[0], own_grads[0], group_size, main, tail)
+    lo_in, lo_up = unpack(lo_sent, main, tail)
+    hi_in, hi_up = unpack(hi_sent, main, tail)
+    far_res, far_grads = expert_split([jnp.concatenate(lo_in, axis=0), jnp.concatenate(hi_in, axis=0)],
+                                      [jnp.concatenate(lo_up, axis=0), jnp.concatenate(hi_up, axis=0)],
+                                      w_gate[0], w_up[0], w_down[0])
+    lo_back = inward(repack(far_res[0], far_grads[0], group_size, main, tail))
+    lo_sum = combine(far_slots, far_w, lo_back.reshape(2 * half_rows, cut), row_slot, first).astype(jnp.bfloat16)
+    near_lo = lax.ppermute(lo_sum, "half", swap)
+    hi_back = inward(repack(far_res[1], far_grads[1], group_size, main, tail))
+    near_lo, hi_back = lax.optimization_barrier((near_lo, hi_back))
+    hi_sum = combine(far_slots, far_w, hi_back.reshape(2 * half_rows, width - cut), row_slot, first).astype(jnp.bfloat16)
+    near_hi = lax.ppermute(hi_sum, "half", swap)
+    near_parts = [near_lo, near_hi]
+    sums = [lo_sum, hi_sum]
+    last, own_packed = lax.optimization_barrier((sums[-1], own_packed))
+    own_back = inward(own_packed)
+    near_part = jnp.concatenate(near_parts, axis=1).astype(jnp.float32)
     own_sum = combine(own_slots, combine_w, own_back.reshape(2 * half_rows, width), row_slot, first) + near_part
     return (own_sum[:token_count].astype(jnp.bfloat16), own_sum[token_count:].astype(jnp.bfloat16))
 

time: 525 us -> 473 us (0.901)
  waiting for transfers between devices: 365 us -> 286 us
  starting transfers between devices: 30.5 us -> 55.7 us
  matrix products: 74.9 us -> 81.1 us
    ppermute x2 -> x4, waiting for transfers between devices: 189 us -> 84.7 us  [the longest x1 52.5 us: per_device(): lax.ppermute(jnp.concatenate([tokens[:, cut:], grad_out[:, cut:]], axis=0...]
    all_to_all x4 -> x6, starting transfers between devices: 19.2 us -> 42.6 us  [inward(): lax.all_to_all(buffer, ('node', 'sub'), split_axis=0, concat_axis=0, tile...]
    ppermute x1, waiting for transfers between devices: 59.2 us -> 81 us  [per_device(): far_w = lax.ppermute(combine_w, 'half', swap)]
    all_to_all x4 -> x6, waiting for transfers between devices: 116 us -> 120 us  [inward(): lax.all_to_all(buffer, ('node', 'sub'), split_axis=0, concat_axis=0, tile...]
    dot_general x2 -> x3, matrix products: 17 us -> 20.1 us  [combine(): summed = jnp.dot(parts, returned, preferred_element_type=jnp.float32)]
    concatenate x2 -> x3, other arithmetic: 11 us -> 9.14 us  [repack(): return jnp.concatenate(pieces, axis=1)]
    slice x5 -> x8, local copies, waits for them, and re-layouts: 9 us -> 10.5 us  [the longest x3 7.53 us: unpack(): inputs = [received[:, :main].reshape(group_size * main, width)]]
    dot_general x6 -> x18, matrix products: 50.1 us -> 51.2 us  [the longest x3 11.5 us: expert_split(): jnp.dot(x, up_w[a:b], preferred_element_type=jnp.float32)]
  transfers between devices with their start and end apart: 8 -> 12, of which waited for: 5 -> 8; matrix products, arithmetic and copies ran while one was open for 8% -> 18% of each run, Pallas kernels for 0% -> 0%
where the time goes in v6:
time: 473 us
  waiting for transfers between devices  286 us (60%)
  matrix products  81.1 us (17%)
  starting transfers between devices  55.7 us (12%)
  local copies, waits for them, and re-layouts  30.2 us (6%)
  other arithmetic  18.1 us (4%)
    all_to_all x6, waiting for transfers between devices, inward(): lax.all_to_all(buffer, ('node', 'sub'), split_axis=0, concat_axis=0, tile...  120 us
    ppermute x1, waiting for transfers between devices, per_device(): far_w = lax.ppermute(combine_w, 'half', swap)  81 us
    ppermute x1, waiting for transfers between devices, per_device(): lax.ppermute(jnp.concatenate([tokens[:, cut:], grad_out[:, cut:]], axis=0...  52.5 us
    all_to_all x6, starting transfers between devices, inward(): lax.all_to_all(buffer, ('node', 'sub'), split_axis=0, concat_axis=0, tile...  42.6 us
    ppermute x1, waiting for transfers between devices, per_device(): near_lo = lax.ppermute(lo_sum, 'half', swap)  32.1 us
    dot_general x3, matrix products, combine(): summed = jnp.dot(parts, returned, preferred_element_type=jnp.float32)  20.1 us
    dot_general x3, matrix products, expert_split(): jnp.dot(x, up_w[a:b], preferred_element_type=jnp.float32)  11.5 us
    dot_general x3, matrix products, pack(): jnp.dot(dispatch, source, preferred_element_type=jnp.float32)  9.84 us
  transfers between devices with their start and end apart: 12, of which 8 were waited for; matrix products, arithmetic and copies ran while one was open for 18% of the time, Pallas kernels for 0%

profile of v6, /device:TPU:0, one launch (start us, length us, event | category | flops | bytes accessed | tf_op | source)
XLA Modules:
  0.0 473.0 jit_solution(9519513018495815191)
XLA Ops:
  1.6 4.1 collective-permute-start
  16.0 4.6 all-to-all-start
  24.7 81.0 %collective-permute-done.2 = f32[128,4]{0,1:T(4,128)S(1)} collective-permute-done((f32[128,4]{0,1:T(4,128)S(1)}, f32[128,4]{0,1:T(4,128)S(1)}, u32[]{:S(2)}, u32[]{:S(2)}) %collective-permute-start.2) | collective-permute-done | bytes 2080 | tf_op jit(solution)/shard_map/ppermute | solution.py:139
  108.0 6.9 %all-to-all-start.1 = ((bf16[16,40,2048]{2,1,0:T(8,128)(2,1)}), bf16[16,40,2048]{2,1,0:T(8,128)(2,1)S(1)}, u32[]{:S(2)}, u32[]{:S(2)}) async-start(bf16[16,40,2048]{2,1,0:T(8,128)(2,1)} %bitcast.133), calls=%async_computation.1 | async-start | bytes 5242880 | tf_op jit(solution)/shard_map/all_to_all | solution.py:30
  116.4 52.5 %collective-permute-done.3 = bf16[256,2048]{1,0:T(8,128)(2,1)} collective-permute-done((bf16[256,2048]{1,0:T(8,128)(2,1)S(1)}, bf16[256,2048]{1,0:T(8,128)(2,1)}, u32[]{:S(2)}, u32[]{:S(2)}) %collective-permute-start.3) | collective-permute-done | bytes 1048608 | tf_op jit(solution)/shard_map/ppermute | solution.py:137
  173.2 4.7 all-to-all-start.2
  183.5 28.1 %all-to-all-done.2 = bf16[16,40,2048]{2,1,0:T(8,128)(2,1)} async-done(((bf16[16,40,2048]{2,1,0:T(8,128)(2,1)}), bf16[16,40,2048]{2,1,0:T(8,128)(2,1)}, u32[]{:S(2)}, u32[]{:S(2)}) %all-to-all-start.2) | async-done | bytes 2621472 | tf_op jit(solution)/shard_map/all_to_all | solution.py:30
  231.8 17.2 %all-to-all-start.3 = ((bf16[16,40,2048]{2,1,0:T(8,128)(2,1)}), bf16[16,40,2048]{2,1,0:T(8,128)(2,1)}, u32[]{:S(2)}, u32[]{:S(2)}) async-start(bf16[16,40,2048]{2,1,0:T(8,128)(2,1)} %pad_maximum_fusion.1), calls=%async_computation.3 | async-start | bytes 5242880 | tf_op jit(solution)/shard_map/all_to_all | solution.py:30
  251.6 4.2 fusion.144
  255.9 7.1 %fusion.6 = f32[320,768]{1,0:T(8,128)} fusion(bf16[1,4096,768]{2,1,0:T(8,128)(2,1)} %param.11, bf16[64,4096]{1,0:T(8,128)(2,1)S(1)} %reshape_squeeze.22, bf16[256,4096]{1,0:T(8,128)(2,1)S(1)} %bitcast.141), kind=kOutput, calls=%fused_computation.7 | convolution fusion | flops 2018508800 | bytes 9895936 | tf_op jit(solution)/shard_map/dot_general | solution.py:104
  270.1 12.4 %all-to-all-done.3 = bf16[16,40,2048]{2,1,0:T(8,128)(2,1)} async-done(((bf16[16,40,2048]{2,1,0:T(8,128)(2,1)}), bf16[16,40,2048]{2,1,0:T(8,128)(2,1)}, u32[]{:S(2)}, u32[]{:S(2)}) %all-to-all-start.3) | async-done | bytes 2621472 | tf_op jit(solution)/shard_map/all_to_all | solution.py:30
  282.5 4.5 all-to-all-start.4
  287.0 6.7 %fusion.2 = f32[320,768]{1,0:T(8,128)} fusion(bf16[1,4096,768]{2,1,0:T(8,128)(2,1)} %param.12, bf16[64,4096]{1,0:T(8,128)(2,1)S(1)} %copy-done.10, bf16[256,4096]{1,0:T(8,128)(2,1)} %bitcast.142), kind=kOutput, calls=%fused_computation.3 | convolution fusion | flops 2018508800 | bytes 9895936 | tf_op jit(solution)/shard_map/dot_general | solution.py:105
  293.9 5.1 %fusion.64 = f32[320,768]{1,0:T(8,128)S(1)} fusion(bf16[64,4096]{1,0:T(8,128)(2,1)S(1)} %reshape_squeeze.23, bf16[256,4096]{1,0:T(8,128)(2,1)S(1)} %bitcast.140, bf16[1,768,4096]{2,1,0:T(8,128)(2,1)} %param.13), kind=kOutput, calls=%fused_computation.58 | convolution fusion | flops 2018508800 | bytes 9895936 | tf_op jit(solution)/shard_map/dot_general | solution.py:106
  299.0 5.1 %fusion = f32[320,4096]{1,0:T(8,128)S(1)} fusion(bf16[1,4096,768]{2,1,0:T(8,128)(2,1)} %param.12, f32[320,768]{1,0:T(8,128)S(1)} %fusion.64, f32[320,768]{1,0:T(8,128)S(1)} %copy-done.12), kind=kOutput, calls=%fused_computation.1 | convolution fusion | flops 2014740480 | bytes 13500416 | tf_op jit(solution)/shard_map/dot_general | solution.py:115
  304.2 5.2 %fusion.11 = bf16[320,4096]{1,0:T(8,128)(2,1)S(1)} fusion(f32[320,4096]{1,0:T(8,128)S(1)} %fusion, bf16[1,4096,768]{2,1,0:T(8,128)(2,1)} %param.11, f32[320,768]{1,0:T(8,128)S(1)} %copy-done.12, f32[320,768]{1,0:T(8,128)S(1)} %fusion.64, f32[320,768]{1,0:T(8,128)S(1)} %copy-done.18), kind=kOutput, calls=%fused_computation.10 | convolution fusion | flops 2018344960 | bytes 17104896 | tf_op jit(solution)/shard_map/dot_general | solution.py:114
  313.0 6.2 %convolution_reduce_fusion.2 = bf16[256,2048]{1,0:T(8,128)(2,1)} fusion(bf16[3,256,640]{2,1,0:T(8,128)(2,1)S(1)} %bitcast.149, bf16[640,2048,1]{1,0,2:T(8,128)(2,1)} %bitcast.23), kind=kOutput, calls=%fused_computation.63 | convolution fusion | flops 2014314496 | bytes 4653056 | tf_op jit(solution)/shard_map/dot_general | solution.py:73
  321.9 5.0 %convolution_convert_fusion.1 = bf16[320,4096]{1,0:T(8,128)(2,1)S(1)} fusion(f32[320,768]{1,0:T(8,128)S(1)} %copy-done.19, f32[320,768]{1,0:T(8,128)S(1)} %copy-done.13, bf16[1,768,4096]{2,1,0:T(8,128)(2,1)} %param.13), kind=kOutput, calls=%fused_computation.11 | convolution fusion | flops 2016051200 | bytes 10878976 | tf_op jit(solution)/shard_map/dot_general | solution.py:113
  330.8 5.3 %pad_maximum_fusion = bf16[16,40,4096]{2,1,0:T(8,128)(2,1)} fusion(bf16[16,4,4096]{2,1,0:T(4,128)(2,1)S(1)} %reshape.267, bf16[16,4,4096]{2,1,0:T(4,128)(2,1)S(1)} %reshape.266, bf16[16,16,4096]{2,1,0:T(8,128)(2,1)S(1)} %bitcast.134, bf16[16,16,4096]{2,1,0:T(8,128)(2,1)} %bitcast.135), kind=kLoop, calls=%fused_computation.12 | loop fusion | flops 20971520 | bytes 10485760 | tf_op jit(solution)/shard_map/concatenate | solution.py:94
  336.1 32.1 %collective-permute-done.4 = bf16[256,2048]{1,0:T(8,128)(2,1)} collective-permute-done((bf16[256,2048]{1,0:T(8,128)(2,1)}, bf16[256,2048]{1,0:T(8,128)(2,1)}, u32[]{:S(2)}, u32[]{:S(2)}) %collective-permute-start.4) | collective-permute-done | bytes 1048608 | tf_op jit(solution)/shard_map/ppermute | solution.py:166
  368.2 5.9 %convolution_reduce_fusion.1 = bf16[256,2048]{1,0:T(8,128)(2,1)} fusion(bf16[3,256,640]{2,1,0:T(8,128)(2,1)} %bitcast.150, bf16[640,2048,1]{1,0,2:T(8,128)(2,1)} %bitcast.27), kind=kOutput, calls=%fused_computation.62 | convolution fusion | flops 2014314496 | bytes 4653056 | tf_op jit(solution)/shard_map/dot_general | solution.py:73
  374.1 4.7 all-to-all-start.5
  382.7 78.7 %all-to-all-done.5 = bf16[16,40,4096]{2,1,0:T(8,128)(2,1)} async-done(((bf16[16,40,4096]{2,1,0:T(8,128)(2,1)}), bf16[16,40,4096]{2,1,0:T(8,128)(2,1)}, u32[]{:S(2)}, u32[]{:S(2)}) %all-to-all-start.5) | async-done | bytes 5242912 | tf_op jit(solution)/shard_map/all_to_all | solution.py:30
  461.4 8.1 %convolution_reduce_fusion = f32[256,4096]{1,0:T(8,128)S(1)} fusion(bf16[3,256,640]{2,1,0:T(8,128)(2,1)S(1)} %bitcast.151, bf16[640,4096,1]{1,0,2:T(8,128)(2,1)} %bitcast.35), kind=kOutput, calls=%fused_computation.14 | convolution fusion | flops 4028628992 | bytes 10420224 | tf_op jit(solution)/shard_map/dot_general | solution.py:73
  (184 shorter events, 75.7 us)
Async XLA Ops:
  0.6 11.4 %copy-start.2 = (bf16[128,4096]{1,0:T(8,128)(2,1)S(1)}, bf16[128,4096]{1,0:T(8,128)(2,1)}, u32[]{:S(2)}) copy-start(bf16[128,4096]{1,0:T(8,128)(2,1)} %param.7) | copy-start | bytes 3145732
  0.6 11.4 %copy-start.1 = (bf16[128,4096]{1,0:T(8,128)(2,1)S(1)}, bf16[128,4096]{1,0:T(8,128)(2,1)}, u32[]{:S(2)}) copy-start(bf16[128,4096]{1,0:T(8,128)(2,1)} %param.8) | copy-start | bytes 3145732
  1.6 7.7 %collective-permute-start = (s32[128,4]{1,0:T(8,128)S(1)}, s32[128,4]{1,0:T(8,128)S(1)}, u32[]{:S(2)}, u32[]{:S(2)}) collective-permute-start(s32[128,4]{1,0:T(8,128)S(1)} %copy.27), channel_id=1, source_target_pairs={{0,4},{4,0},{1,5},{5,1},{2,6},{6,2},{3,7},{7,3},{8,12},{12,8},{9,1... | collective-permute-start | bytes 6152 | tf_op jit(solution)/shard_map/ppermute | solution.py:138
  16.0 89.7 %all-to-all-start = ((bf16[16,40,4096]{2,1,0:T(8,128)(2,1)}), bf16[16,40,4096]{2,1,0:T(8,128)(2,1)}, u32[]{:S(2)}, u32[]{:S(2)}) async-start(bf16[16,40,4096]{2,1,0:T(8,128)(2,1)} %bitcast.131), calls=%async_computation | async-start | bytes 10485760 | tf_op jit(solution)/shard_map/all_to_all | solution.py:30
  21.7 84.0 %collective-permute-start.1 = (bf16[256,2048]{1,0:T(8,128)(2,1)S(1)}, bf16[256,2048]{1,0:T(8,128)(2,1)S(1)}, u32[]{:S(2)}, u32[]{:S(2)}) collective-permute-start(bf16[256,2048]{1,0:T(8,128)(2,1)S(1)} %pad_maximum_fusion.8), channel_id=1, source_target_pairs={{0,4},{4,0},{1,5},{5,1},{2,6},{6,2},{3,7},{7,3},{8,12},{12,8},{9,1... | collective-permute-start | bytes 3145736 | tf_op jit(solution)/shard_map/ppermute | solution.py:136
  24.4 81.3 %collective-permute-start.2 = (f32[128,4]{0,1:T(4,128)S(1)}, f32[128,4]{0,1:T(4,128)S(1)}, u32[]{:S(2)}, u32[]{:S(2)}) collective-permute-start(f32[128,4]{0,1:T(4,128)S(1)} %copy-done.11), channel_id=1, source_target_pairs={{0,4},{4,0},{1,5},{5,1},{2,6},{6,2},{3,7},{7,3},{8,12},{12,8},{9,1... | collective-permute-start | bytes 6152 | tf_op jit(solution)/shard_map/ppermute | solution.py:139
  108.0 61.6 %all-to-all-start.1 = ((bf16[16,40,2048]{2,1,0:T(8,128)(2,1)}), bf16[16,40,2048]{2,1,0:T(8,128)(2,1)S(1)}, u32[]{:S(2)}, u32[]{:S(2)}) async-start(bf16[16,40,2048]{2,1,0:T(8,128)(2,1)} %bitcast.133), calls=%async_computation.1 | async-start | bytes 5242880 | tf_op jit(solution)/shard_map/all_to_all | solution.py:30
  116.1 52.8 %collective-permute-start.3 = (bf16[256,2048]{1,0:T(8,128)(2,1)S(1)}, bf16[256,2048]{1,0:T(8,128)(2,1)}, u32[]{:S(2)}, u32[]{:S(2)}) collective-permute-start(bf16[256,2048]{1,0:T(8,128)(2,1)S(1)} %pad_maximum_fusion.9), channel_id=1, source_target_pairs={{0,4},{4,0},{1,5},{5,1},{2,6},{6,2},{3,7},{7,3},{8,12},{12,8},{9,1... | collective-permute-start | bytes 3145736 | tf_op jit(solution)/shard_map/ppermute | solution.py:137
  173.2 38.4 %all-to-all-start.2 = ((bf16[16,40,2048]{2,1,0:T(8,128)(2,1)}), bf16[16,40,2048]{2,1,0:T(8,128)(2,1)}, u32[]{:S(2)}, u32[]{:S(2)}) async-start(bf16[16,40,2048]{2,1,0:T(8,128)(2,1)} %bitcast.132), calls=%async_computation.2 | async-start | bytes 5242880 | tf_op jit(solution)/shard_map/all_to_all | solution.py:30
  231.8 50.7 %all-to-all-start.3 = ((bf16[16,40,2048]{2,1,0:T(8,128)(2,1)}), bf16[16,40,2048]{2,1,0:T(8,128)(2,1)}, u32[]{:S(2)}, u32[]{:S(2)}) async-start(bf16[16,40,2048]{2,1,0:T(8,128)(2,1)} %pad_maximum_fusion.1), calls=%async_computation.3 | async-start | bytes 5242880 | tf_op jit(solution)/shard_map/all_to_all | solution.py:30
  251.6 11.4 %slice-start.4 = ((s8[6291456]{0:T(1024)(128)(4,1)}), s8[4194304]{0:T(1024)(128)(4,1)S(1)}, s32[]{:S(2)}) async-start(s8[6291456]{0:T(1024)(128)(4,1)} %bitcast.154), calls=%async_computation.10 | async-start | bytes 8388608
  251.6 12.6 %slice-start.8 = ((s8[6291456]{0:T(1024)(128)(4,1)}), s8[4194304]{0:T(1024)(128)(4,1)S(1)}, s32[]{:S(2)}) async-start(s8[6291456]{0:T(1024)(128)(4,1)} %bitcast.158), calls=%async_computation.14 | async-start | bytes 8388608
  255.9 7.1 %copy-start.4 = (bf16[16,16,4096]{2,1,0:T(8,128)(2,1)}, bf16[16,16,4096]{2,1,0:T(8,128)(2,1)S(1)}, u32[]{:S(2)}) copy-start(bf16[16,16,4096]{2,1,0:T(8,128)(2,1)S(1)} %get-tuple-element.22) | copy-start | bytes 6291460
  255.9 7.1 %slice-start.5 = ((s8[6291456]{0:T(1024)(128)(4,1)}), s8[2097152]{0:T(1024)(128)(4,1)S(1)}, s32[]{:S(2)}) async-start(s8[6291456]{0:T(1024)(128)(4,1)} %bitcast.154), calls=%async_computation.11 | async-start | bytes 4194304
  255.9 8.4 %slice-start.9 = ((s8[6291456]{0:T(1024)(128)(4,1)}), s8[2097152]{0:T(1024)(128)(4,1)S(1)}, s32[]{:S(2)}) async-start(s8[6291456]{0:T(1024)(128)(4,1)} %bitcast.158), calls=%async_computation.15 | async-start | bytes 4194304
  270.1 16.9 %copy-start.10 = (bf16[64,4096]{1,0:T(8,128)(2,1)S(1)}, bf16[64,4096]{1,0:T(8,128)(2,1)}, u32[]{:S(2)}) copy-start(bf16[64,4096]{1,0:T(8,128)(2,1)} %copy-done.9) | copy-start | bytes 1572868
  282.5 53.6 %all-to-all-start.4 = ((bf16[16,40,2048]{2,1,0:T(8,128)(2,1)}), bf16[16,40,2048]{2,1,0:T(8,128)(2,1)}, u32[]{:S(2)}, u32[]{:S(2)}) async-start(bf16[16,40,2048]{2,1,0:T(8,128)(2,1)} %pad_maximum_fusion.2), calls=%async_computation.4 | async-start | bytes 5242880 | tf_op jit(solution)/shard_map/all_to_all | solution.py:30
  287.0 6.9 %copy-start.3 = (bf16[16,16,4096]{2,1,0:T(8,128)(2,1)S(1)}, bf16[16,16,4096]{2,1,0:T(8,128)(2,1)}, u32[]{:S(2)}) copy-start(bf16[16,16,4096]{2,1,0:T(8,128)(2,1)} %get-tuple-element.23) | copy-start | bytes 6291460
  313.0 8.9 %copy-start.13 = (f32[320,768]{1,0:T(8,128)S(1)}, f32[320,768]{1,0:T(8,128)}, u32[]{:S(2)}) copy-start(f32[320,768]{1,0:T(8,128)} %fusion.6) | copy-start | bytes 2949124
  313.0 8.9 %copy-start.19 = (f32[320,768]{1,0:T(8,128)S(1)}, f32[320,768]{1,0:T(8,128)}, u32[]{:S(2)}) copy-start(f32[320,768]{1,0:T(8,128)} %fusion.2) | copy-start | bytes 2949124
  319.2 49.1 %collective-permute-start.4 = (bf16[256,2048]{1,0:T(8,128)(2,1)}, bf16[256,2048]{1,0:T(8,128)(2,1)}, u32[]{:S(2)}, u32[]{:S(2)}) collective-permute-start(bf16[256,2048]{1,0:T(8,128)(2,1)} %convolution_reduce_fusion.2), channel_id=1, source_target_pairs={{0,4},{4,0},{1,5},{5,1},{2,6},{6,2},{3,7},{7,3},{8,12},{12,8},{9,1... | collective-permute-start | bytes 3145736 | tf_op jit(solution)/shard_map/ppermute | solution.py:166
  374.1 7.8 %copy-start.5 = (f32[128,640]{0,1:T(8,128)S(1)}, f32[128,640]{0,1:T(8,128)}, u32[]{:S(2)}) copy-start(f32[128,640]{0,1:T(8,128)} %get-tuple-element.60) | copy-start | bytes 983044
  374.1 87.3 %all-to-all-start.5 = ((bf16[16,40,4096]{2,1,0:T(8,128)(2,1)}), bf16[16,40,4096]{2,1,0:T(8,128)(2,1)}, u32[]{:S(2)}, u32[]{:S(2)}) async-start(bf16[16,40,4096]{2,1,0:T(8,128)(2,1)} %pad_maximum_fusion), calls=%async_computation.5 | async-start | bytes 10485760 | tf_op jit(solution)/shard_map/all_to_all | solution.py:30
  378.8 90.7 %collective-permute-start.5 = (bf16[256,2048]{1,0:T(8,128)(2,1)}, bf16[256,2048]{1,0:T(8,128)(2,1)S(1)}, u32[]{:S(2)}, u32[]{:S(2)}) collective-permute-start(bf16[256,2048]{1,0:T(8,128)(2,1)} %convolution_reduce_fusion.1), channel_id=1, source_target_pairs={{0,4},{4,0},{1,5},{5,1},{2,6},{6,2},{3,7},{7,3},{8,12},{12,8},{9,1... | collective-permute-start | bytes 3145736 | tf_op jit(solution)/shard_map/ppermute | solution.py:170
  (22 other events, 65.9 us)
